TPU v7x, 128 devices: a whole 4x4x4 slice. The times are simulated.
128 devices in a mesh: section: 2 (over core), seq: 4 (over x), tensor: 16 (over z, y).
Axes of the slice: x: 4, y: 4, z: 4, core: 2. Of those that a mesh axis runs over, the one named last changes fastest.
Arguments:
- queries: bfloat16 [2560, 8192], P(('section', 'seq'), 'tensor'), may hold values from -200 to 200
- neighbours: bfloat16 [10240, 8192], P(('section', 'seq', 'tensor')), may hold values from -6 to 6
- kv_weight: bfloat16 [2, 8192, 8192], P(None, None, 'tensor'), may hold values from -0.0625 to 0.0625
- out_weight: bfloat16 [8192, 8192], P('tensor'), may hold values from -0.5 to 0.5
- slot_map: int32 [40], replicated, may hold values from 0 to 39, as said below
Outputs:
- mixed: bfloat16 [2560, 8192], P(('section', 'seq', 'tensor'))
Inputs may be any that keep to these rules, and one draw needn't show every extreme that they name: `slot_map`: distinct numbers; slot s lies on encoder shard s // 5; at most 2 spans of one sequence shard map to one encoder shard, and that many do for some pair of shards.
All inputs are finite; a program needn't handle non-finite values.
Results may differ from a plain program's by a relative error of at most 0.013.
Values may be sent and summed in bfloat16 or wider, within the bound.
No kernel may reach another device: no remote copies, remote signals or barrier semaphores. Data moves between devices by JAX's collectives and lax.ppermute only.
A program may use at most 128 MiB of HBM per device.

v0:
```python
import math

import jax
import jax.numpy as jnp
from jax import lax
from jax.sharding import PartitionSpec as P

HD = 128
SPAN = 64
PEER = 2
CH_DEV = 5
CAPC = 5
KEYS = 256


def attend(query_block, key_values):
    scores = jnp.einsum(
        "bqhd,bkhd->bhqk", query_block, key_values[:, :, 0], preferred_element_type=jnp.float32
    )
    scores = scores * (1.0 / math.sqrt(HD))
    peak = jnp.max(scores, axis=-1, keepdims=True)
    expo = jnp.exp(scores - peak)
    weights = (expo / jnp.sum(expo, axis=-1, keepdims=True)).astype(jnp.bfloat16)
    result = jnp.einsum(
        "bhqk,bkhd->bqhd", weights, key_values[:, :, 1], preferred_element_type=jnp.float32
    )
    return result.astype(jnp.bfloat16)


def on_device(queries, neighbours, kv_weight, out_weight, slot_map):
    groups = lax.axis_size(("section", "seq"))
    group_index = lax.axis_index(("section", "seq"))
    heads_local = kv_weight.shape[2] // HD
    per_peer = PEER
    spans = slot_map.shape[0]
    row_block = lax.all_gather(neighbours, "tensor", axis=0, tiled=True)
    result = jnp.einsum("rd,kde->rke", row_block, kv_weight, preferred_element_type=jnp.float32)
    projected = result.astype(jnp.bfloat16).reshape(row_block.shape[0], 2 * kv_weight.shape[2])
    slot_values = projected.reshape(CAPC, KEYS, 2, heads_local, HD)
    span_ids = jnp.arange(spans, dtype=jnp.int32)
    owner_shard = slot_map // CAPC
    slot_index = slot_map % CAPC
    seq_owner = span_ids // CH_DEV
    earlier = (seq_owner[:, None] == seq_owner[None, :]) & (
        owner_shard[:, None] == owner_shard[None, :]
    )
    earlier = earlier & (span_ids[None, :] < span_ids[:, None])
    arrival = jnp.sum(earlier.astype(jnp.int32), axis=1)
    target_ids = jnp.arange(groups, dtype=jnp.int32)[:, None, None]
    place_ids = jnp.arange(per_peer, dtype=jnp.int32)[None, :, None]
    selection = (seq_owner[None, None, :] == target_ids) & (arrival[None, None, :] == place_ids)
    selection = selection & (owner_shard[None, None, :] == group_index)
    send_slot = jnp.sum(jnp.where(selection, slot_index[None, None, :], 0), axis=-1)
    occupied = jnp.any(selection, axis=-1)
    own_shards = lax.dynamic_slice_in_dim(owner_shard, group_index * CH_DEV, CH_DEV)
    own_arrival = lax.dynamic_slice_in_dim(arrival, group_index * CH_DEV, CH_DEV)
    own_place = own_shards * per_peer + own_arrival
    query_blocks = queries.reshape(CH_DEV, SPAN, heads_local, HD)
    local_pairs = jnp.where(
        occupied[:, :, None, None, None, None], slot_values[send_slot], jnp.zeros((), jnp.bfloat16)
    )
    received = lax.all_to_all(
        local_pairs, ("section", "seq"), split_axis=0, concat_axis=0, tiled=True
    )
    key_values = received.reshape(groups * per_peer, KEYS, 2, heads_local, HD)[own_place]
    attended = attend(query_blocks, key_values)
    attended_flat = attended.reshape(CH_DEV * SPAN, heads_local * HD)
    mixed = lax.psum_scatter(
        jnp.dot(attended_flat, out_weight, preferred_element_type=jnp.float32),
        "tensor",
        scatter_dimension=0,
        tiled=True,
    )
    return mixed.astype(jnp.bfloat16)


def solution(mesh):
    placed = (
        P(("section", "seq"), "tensor"),
        P(("section", "seq", "tensor"), None),
        P(None, None, "tensor"),
        P("tensor", None),
        P(),
    )
    return jax.shard_map(
        on_device,
        mesh=mesh,
        in_specs=placed,
        out_specs=P(("section", "seq", "tensor"), None),
        check_vma=False,
    )
```

profile of v0, /device:TPU:0, one launch (start us, length us, event | category | flops | bytes accessed | tf_op | source)
XLA Modules:
  0.0 552.7 jit_solution(7348434239065273170)
XLA Ops:
  6.5 0.0 all-gather.2.cloned.1.call-start
  6.5 0.7 all-gather.2.cloned.1.call-update
  7.3 0.7 broadcast_compare_fusion
  8.0 0.2 convert_reduce_fusion
  8.1 0.7 and_select_fusion
  8.8 0.1 select_reduce_fusion
  9.0 0.1 copy.21
  9.1 0.1 reshape.121
  9.1 0.2 fusion.18
  9.3 0.1 copy.20
  9.4 135.4 %all-gather.2.cloned.1.call-done = bf16[1280,8192]{1,0:T(8,128)(2,1)} async-done(((bf16[80,8192]{1,0:T(8,128)(2,1)}), bf16[1280,8192]{1,0:T(8,128)(2,1)}) %all-gather.2.cloned.1.call-update) | async-done | bytes 20971536 | tf_op jit(solution)/shard_map/all_gather | solution.py:36
  144.8 28.1 %fusion.3 = bf16[1280,2,512]{2,0,1:T(8,128)(2,1)} fusion(bf16[2,8192,512]{2,1,0:T(8,128)(2,1)} %param.7, bf16[1280,8192]{1,0:T(8,128)(2,1)} %all-gather.2.cloned.1.call-done), kind=kOutput, calls=%fused_computation.6 | convolution fusion | flops 21476147200 | bytes 40370176 | tf_op jit(solution)/shard_map/rd,kde->rke/dot_general | solution.py:37
  172.8 3.5 reshape_reshape.3
  176.4 8.9 %gather_fusion = bf16[16,256,2,4,128]{4,3,1,2,0:T(4,128)(2,1)} fusion(bf16[5,256,2,4,128]{4,3,1,0,2:T(4,128)(2,1)S(1)} %reshape_reshape.3, s32[1024]{0:T(1024)S(1)} %pad_clamp_fusion.1), kind=kCustom, calls=%fused_computation | custom fusion | bytes 16777280 | tf_op jit(solution)/shard_map/gather | solution.py:60
  185.3 7.7 %copy_select_fusion = bf16[8,2,256,2,4,128]{5,2,4,3,1,0:T(8,128)(2,1)} fusion(bf16[8,2,256,2,4,128]{5,4,2,3,1,0:T(4,128)(2,1)} %bitcast.41, pred[8,2]{1,0:T(8,128)(4,1)S(1)} %copy.20), kind=kLoop, calls=%fused_computation.5 | loop fusion | flops 4194304 | bytes 16777232 | tf_op jit(solution)/shard_map/jit(_where)/select_n | solution.py:59
  193.0 5.4 all-to-all-start
  198.3 0.0 copy-done.1
  198.4 0.1 reshape.117
  198.4 0.0 copy-done.2
  198.5 0.6 dynamic-slice
  199.7 0.1 compare_select_fusion.1
  199.8 92.3 %all-to-all-done = bf16[8,2,256,2,4,128]{5,2,4,3,1,0:T(8,128)(2,1)} async-done(((bf16[8,2,256,2,4,128]{5,2,4,3,1,0:T(8,128)(2,1)}), bf16[8,2,256,2,4,128]{5,2,4,3,1,0:T(8,128)(2,1)}, u32[]{:S(2)}, u32[]{:S(2)}) %all-to-all-start) | async-done | bytes 8388640 | tf_op jit(solution)/shard_map/all_to_all | solution.py:62
  292.1 4.4 gather_fusion.1
  296.5 0.6 fusion.8
  297.1 0.0 copy-start
  297.1 1.1 copy-done
  298.1 0.4 fusion.20
  298.6 4.0 fusion.11
  302.6 0.3 copy.26
  302.9 8.9 %fusion.13 = f32[320,8192]{1,0:T(8,128)} fusion(bf16[512,8192]{1,0:T(8,128)(2,1)} %param.8, bf16[40,8,4,128]{3,2,1,0:T(4,128)(2,1)S(1)} %bitcast.42), kind=kOutput, calls=%fused_computation.19 | convolution fusion | flops 2684354560 | bytes 19202048 | tf_op jit(solution)/shard_map/dot_general | solution.py:69
  311.8 232.1 %all-reduce.2 = bf16[320,8192]{1,0:T(8,128)(2,1)} all-reduce(f32[320,8192]{1,0:T(8,128)} %fusion.13), channel_id=2, replica_groups=mesh['section'=2,'seq'=4,'tensor'=16] {'tensor'}, use_global_device_ids=true, to_apply=%region_5.6.clone | all-reduce | flops 2621440 | bytes 15728640
  543.9 1.9 dynamic-slice_convert_fusion
  (8 shorter events, 0.0 us)
Async XLA Ops:
  6.5 138.2 %all-gather.2.cloned.1.call-start = ((), (), s32[]{:S(2)}) async-start(), calls=%async_computation.1 | async-start | bytes 22282240 | tf_op jit(solution)/shard_map/all_gather | solution.py:36
  193.0 5.4 copy-start.1
  193.0 5.5 copy-start.2
  193.0 99.1 %all-to-all-start = ((bf16[8,2,256,2,4,128]{5,2,4,3,1,0:T(8,128)(2,1)}), bf16[8,2,256,2,4,128]{5,2,4,3,1,0:T(8,128)(2,1)}, u32[]{:S(2)}, u32[]{:S(2)}) async-start(bf16[8,2,256,2,4,128]{5,2,4,3,1,0:T(8,128)(2,1)} %copy_select_fusion), calls=%async_computation | async-start | bytes 16777216 | tf_op jit(solution)/shard_map/all_to_all | solution.py:62
  297.1 1.1 copy-start
Sparse Core Ops, SparseCore 0:
  9.5 135.2 all-gather.1
where the time goes:
time: 553 us
  blocking collectives  232 us (42%)
  waiting for transfers between devices  228 us (41%)
  matrix products  41.6 us (8%)
  local copies, waits for them, and re-layouts  21 us (4%)
  between operations  14.2 us (3%)
  other arithmetic  10.1 us (2%)
    unnamed x1, blocking collectives  232 us
    all_gather x1, waiting for transfers between devices, on_device(): row_block = lax.all_gather(neighbours, 'tensor', axis=0, tiled=True)  135 us
    all_to_all x1, waiting for transfers between devices, on_device(): lax.all_to_all(local_pairs, ('section', 'seq'), split_axis=0, concat_axis...  92.3 us
    dot_general x1, matrix products, on_device(): jnp.einsum('rd,kde->rke', row_block, kv_weight, preferred_element_type=jn...  28.1 us
  transfers between devices with their start and end apart: 2, of which 2 were waited for; matrix products, arithmetic and copies ran while one was open for 1% of the time, Pallas kernels for 0%

commit v1 on v0

v1 whole, which is shorter than its diff:
```python
import math

import jax
import jax.numpy as jnp
from jax import lax
from jax.sharding import PartitionSpec as P

HD = 128
SPAN = 64
PEER = 2
CH_DEV = 5
CAPC = 5
KEYS = 256
ROW_CHUNKS = 5


def attend(query_block, keys, values):
    scores = jnp.einsum(
        "bqhd,bkhd->bhqk", query_block, keys, preferred_element_type=jnp.float32
    )
    scores = scores * (1.0 / math.sqrt(HD))
    peak = jnp.max(scores, axis=-1, keepdims=True)
    expo = jnp.exp(scores - peak)
    weights = (expo / jnp.sum(expo, axis=-1, keepdims=True)).astype(jnp.bfloat16)
    result = jnp.einsum(
        "bhqk,bkhd->bqhd", weights, values, preferred_element_type=jnp.float32
    )
    return result.astype(jnp.bfloat16)


def on_device(queries, neighbours, kv_weight, out_weight, slot_map):
    groups = lax.axis_size(("section", "seq"))
    group_index = lax.axis_index(("section", "seq"))
    tensor_size = lax.axis_size("tensor")
    cols = kv_weight.shape[2]
    heads_local = cols // HD
    spans = slot_map.shape[0]
    rows_local = neighbours.shape[0]

    span_ids = jnp.arange(spans, dtype=jnp.int32)
    owner_shard = slot_map // CAPC
    slot_index = slot_map % CAPC
    seq_owner = span_ids // CH_DEV
    earlier = (seq_owner[:, None] == seq_owner[None, :]) & (
        owner_shard[:, None] == owner_shard[None, :]
    )
    earlier = earlier & (span_ids[None, :] < span_ids[:, None])
    arrival = jnp.sum(earlier.astype(jnp.int32), axis=1)

    peer_ids = jnp.arange(groups, dtype=jnp.int32)[:, None, None]
    place_ids = jnp.arange(PEER, dtype=jnp.int32)[None, :, None]

    own_spans = group_index * CH_DEV + jnp.arange(CH_DEV, dtype=jnp.int32)
    own_owner = owner_shard[own_spans]
    own_arrival = arrival[own_spans]
    pick_q = (own_owner[None, None, :] == peer_ids) & (own_arrival[None, None, :] == place_ids)
    send_q_idx = jnp.sum(
        jnp.where(pick_q, jnp.arange(CH_DEV, dtype=jnp.int32)[None, None, :], 0), axis=-1
    )
    query_blocks = queries.reshape(CH_DEV, SPAN, cols)
    send_q = query_blocks[send_q_idx]
    recv_q = lax.all_to_all(send_q, ("section", "seq"), split_axis=0, concat_axis=0, tiled=True)

    my_slots = group_index * CAPC + jnp.arange(CAPC, dtype=jnp.int32)
    hit = slot_map[None, :] == my_slots[:, None]
    slot_span = jnp.sum(jnp.where(hit, span_ids[None, :], 0), axis=1)
    slot_group = slot_span // CH_DEV
    slot_place = arrival[slot_span]
    q_for_slot = recv_q[slot_group, slot_place].reshape(CAPC, SPAN, heads_local, HD)

    sub = rows_local // ROW_CHUNKS
    nb_chunks = neighbours.reshape(ROW_CHUNKS, sub, neighbours.shape[1])
    kv_parts = []
    for i in range(ROW_CHUNKS):
        rows = lax.all_gather(nb_chunks[i], "tensor", axis=0, tiled=True)
        part = jnp.einsum("rd,kde->rke", rows, kv_weight, preferred_element_type=jnp.float32)
        kv_parts.append(part.astype(jnp.bfloat16).reshape(tensor_size, sub, 2, cols))
    kv = jnp.stack(kv_parts, axis=1).reshape(tensor_size * rows_local, 2, cols)
    kv = kv.reshape(CAPC, KEYS, 2, heads_local, HD)
    attended = attend(q_for_slot, kv[:, :, 0], kv[:, :, 1]).reshape(CAPC, SPAN, cols)

    pick_a = (slot_group[None, None, :] == peer_ids) & (slot_place[None, None, :] == place_ids)
    send_a_idx = jnp.sum(
        jnp.where(pick_a, jnp.arange(CAPC, dtype=jnp.int32)[None, None, :], 0), axis=-1
    )
    send_a = attended[send_a_idx]
    recv_a = lax.all_to_all(send_a, ("section", "seq"), split_axis=0, concat_axis=0, tiled=True)
    attended_flat = recv_a[own_owner, own_arrival].reshape(CH_DEV * SPAN, cols)

    partial = jnp.dot(attended_flat, out_weight, preferred_element_type=jnp.float32)
    partial = partial.astype(jnp.bfloat16).reshape(tensor_size, -1, out_weight.shape[1])
    mixed = lax.psum_scatter(partial, "tensor", scatter_dimension=0, tiled=True)
    return mixed.reshape(-1, out_weight.shape[1])


def solution(mesh):
    placed = (
        P(("section", "seq"), "tensor"),
        P(("section", "seq", "tensor"), None),
        P(None, None, "tensor"),
        P("tensor", None),
        P(),
    )
    return jax.shard_map(
        on_device,
        mesh=mesh,
        in_specs=placed,
        out_specs=P(("section", "seq", "tensor"), None),
        check_vma=False,
    )
```

time: 553 us -> 424 us (0.77)
  blocking collectives: 232 us -> 0 us
  waiting for transfers between devices: 228 us -> 304 us
  matrix products: 41.6 us -> 68.7 us
  other arithmetic: 10.1 us -> 1.39 us
  local copies, waits for them, and re-layouts: 21 us -> 26.9 us
    unnamed x1 -> x0, blocking collectives: 232 us -> none
    unnamed x1 -> x7, waiting for transfers between devices: 0.71 us -> 83.2 us
    all_to_all x1 -> x2, waiting for transfers between devices: 92.3 us -> 28.7 us  [the longest x1 15.2 us: on_device(): lax.all_to_all(send_a, ('section', 'seq'), split_axis=0, concat_axis=0, t...]
    all_gather x1 -> x5, waiting for transfers between devices: 135 us -> 192 us  [on_device(): rows = lax.all_gather(nb_chunks[i], 'tensor', axis=0, tiled=True)]
    dot_general x3 -> x7, matrix products: 32.7 us -> 60.7 us  [the longest x5 57.8 us: on_device(): jnp.einsum('rd,kde->rke', rows, kv_weight, preferred_element_type=jnp.flo...]
    select_n x4 -> x5, other arithmetic: 8.47 us -> 0.04 us  [the longest x1 0.01 us: on_device(): slot_group = slot_span // CH_DEV]
    reshape x1 -> x2, local copies, waits for them, and re-layouts: 0.08 us -> 7.73 us  [the longest x1 7.67 us: on_device(): partial.astype(jnp.bfloat16).reshape(tensor_size, -1, out_weight.shape[1])]
    gather x2 -> x7, local copies, waits for them, and re-layouts: 13.3 us -> 6.25 us  [the longest x1 1.59 us: on_device(): send_q = query_blocks[send_q_idx]]
  transfers between devices with their start and end apart: 2 -> 8, of which waited for: 2 -> 8; matrix products, arithmetic and copies ran while one was open for 1% -> 13% of each run, Pallas kernels for 0% -> 0%
where the time goes in v1:
time: 424 us; the launch traced here: 423 us
  waiting for transfers between devices  304 us (72%)
  matrix products  68.7 us (16%)
  local copies, waits for them, and re-layouts  26.9 us (6%)
  between operations  13.6 us (3%)
  starting transfers between devices  8.86 us (2%)
    all_gather x5, waiting for transfers between devices, on_device(): rows = lax.all_gather(nb_chunks[i], 'tensor', axis=0, tiled=True)  192 us
    unnamed x7, waiting for transfers between devices  83.2 us
    dot_general x5, matrix products, on_device(): jnp.einsum('rd,kde->rke', rows, kv_weight, preferred_element_type=jnp.flo...  57.8 us
    all_to_all x1, waiting for transfers between devices, on_device(): lax.all_to_all(send_a, ('section', 'seq'), split_axis=0, concat_axis=0, t...  15.2 us
    all_to_all x1, waiting for transfers between devices, on_device(): lax.all_to_all(send_q, ('section', 'seq'), split_axis=0, concat_axis=0, t...  13.6 us
  transfers between devices with their start and end apart: 8, of which 8 were waited for; matrix products, arithmetic and copies ran while one was open for 13% of the time, Pallas kernels for 0%

profile of v1, /device:TPU:0, one launch (start us, length us, event | category | flops | bytes accessed | tf_op | source)
XLA Modules:
  0.0 423.1 jit_solution(17745739892705886127)
XLA Ops:
  6.5 2.4 fusion.53
  9.0 0.7 all-gather.8.cloned.1.call-update
  9.8 0.7 all-gather.10.cloned.1.call-update
  11.3 0.6 gather_fusion
  12.1 0.6 gather_fusion.1
  13.2 1.6 gather_fusion.2
  14.8 4.4 %all-to-all-start = ((bf16[8,2,64,512]{3,2,1,0:T(8,128)(2,1)}), bf16[8,2,64,512]{3,2,1,0:T(8,128)(2,1)S(1)}, u32[]{:S(2)}, u32[]{:S(2)}) async-start(bf16[8,2,64,512]{3,2,1,0:T(8,128)(2,1)} %bitcast.19), calls=%async_computation | async-start | bytes 2097152 | tf_op jit(solution)/shard_map/all_to_all | solution.py:62
  20.9 13.6 %all-to-all-done = bf16[8,2,64,512]{3,2,1,0:T(8,128)(2,1)S(1)} async-done(((bf16[8,2,64,512]{3,2,1,0:T(8,128)(2,1)}), bf16[8,2,64,512]{3,2,1,0:T(8,128)(2,1)S(1)}, u32[]{:S(2)}, u32[]{:S(2)}) %all-to-all-start) | async-done | bytes 1048608 | tf_op jit(solution)/shard_map/all_to_all | solution.py:62
  35.0 28.5 %all-gather.6.cloned.1.call-done = bf16[256,8192]{1,0:T(8,128)(2,1)} async-done(((bf16[16,8192]{1,0:T(8,128)(2,1)}), bf16[256,8192]{1,0:T(8,128)(2,1)}) %all-gather.6.cloned.1.call-update) | async-done | bytes 4194320 | tf_op jit(solution)/shard_map/all_gather | solution.py:75
  63.5 11.5 %fusion.14 = bf16[256,2,512]{2,0,1:T(8,128)(2,1)S(1)} fusion(bf16[2,8192,512]{2,1,0:T(8,128)(2,1)} %param.7, bf16[256,8192]{1,0:T(8,128)(2,1)} %all-gather.6.cloned.1.call-done), kind=kOutput, calls=%fused_computation.26 | convolution fusion | flops 4295229440 | bytes 21495808 | tf_op jit(solution)/shard_map/rd,kde->rke/dot_general | solution.py:76
  75.1 0.9 constant_dynamic-update-slice_fusion.4
  76.0 40.9 %all-gather.8.cloned.1.call-done = bf16[256,8192]{1,0:T(8,128)(2,1)} async-done(((bf16[16,8192]{1,0:T(8,128)(2,1)}), bf16[256,8192]{1,0:T(8,128)(2,1)}) %all-gather.8.cloned.1.call-update) | async-done | bytes 4194320 | tf_op jit(solution)/shard_map/all_gather | solution.py:75
  116.8 11.5 %fusion.17 = bf16[256,2,512]{2,0,1:T(8,128)(2,1)S(1)} fusion(bf16[2,8192,512]{2,1,0:T(8,128)(2,1)} %param.7, bf16[256,8192]{1,0:T(8,128)(2,1)} %all-gather.8.cloned.1.call-done), kind=kOutput, calls=%fused_computation.27 | convolution fusion | flops 4295229440 | bytes 21495808 | tf_op jit(solution)/shard_map/rd,kde->rke/dot_general | solution.py:76
  128.3 0.8 constant_dynamic-update-slice_fusion.3
  129.2 40.9 %all-gather.10.cloned.1.call-done = bf16[256,8192]{1,0:T(8,128)(2,1)} async-done(((bf16[16,8192]{1,0:T(8,128)(2,1)}), bf16[256,8192]{1,0:T(8,128)(2,1)}) %all-gather.10.cloned.1.call-update) | async-done | bytes 4194320 | tf_op jit(solution)/shard_map/all_gather | solution.py:75
  170.1 11.5 %fusion.20 = bf16[256,2,512]{2,0,1:T(8,128)(2,1)S(1)} fusion(bf16[2,8192,512]{2,1,0:T(8,128)(2,1)} %param.7, bf16[256,8192]{1,0:T(8,128)(2,1)} %all-gather.10.cloned.1.call-done), kind=kOutput, calls=%fused_computation.28 | convolution fusion | flops 4295229440 | bytes 21495808 | tf_op jit(solution)/shard_map/rd,kde->rke/dot_general | solution.py:76
  181.6 0.9 constant_dynamic-update-slice_fusion.2
  182.5 40.7 %all-gather.12.cloned.1.call-done = bf16[256,8192]{1,0:T(8,128)(2,1)} async-done(((bf16[16,8192]{1,0:T(8,128)(2,1)}), bf16[256,8192]{1,0:T(8,128)(2,1)}) %all-gather.12.cloned.1.call-update) | async-done | bytes 4194320 | tf_op jit(solution)/shard_map/all_gather | solution.py:75
  223.2 11.5 %fusion.23 = bf16[256,2,512]{2,0,1:T(8,128)(2,1)S(1)} fusion(bf16[2,8192,512]{2,1,0:T(8,128)(2,1)} %param.7, bf16[256,8192]{1,0:T(8,128)(2,1)} %all-gather.12.cloned.1.call-done), kind=kOutput, calls=%fused_computation.29 | convolution fusion | flops 4295229440 | bytes 21495808 | tf_op jit(solution)/shard_map/rd,kde->rke/dot_general | solution.py:76
  234.7 0.9 constant_dynamic-update-slice_fusion.1
  235.6 40.7 %all-gather.14.cloned.1.call-done = bf16[256,8192]{1,0:T(8,128)(2,1)} async-done(((bf16[16,8192]{1,0:T(8,128)(2,1)}), bf16[256,8192]{1,0:T(8,128)(2,1)}) %all-gather.14.cloned.1.call-update) | async-done | bytes 4194320 | tf_op jit(solution)/shard_map/all_gather | solution.py:75
  276.3 11.7 %fusion.26 = bf16[256,2,512]{2,0,1:T(8,128)(2,1)S(1)} fusion(bf16[2,8192,512]{2,1,0:T(8,128)(2,1)} %param.7, bf16[256,8192]{1,0:T(8,128)(2,1)} %all-gather.14.cloned.1.call-done), kind=kOutput, calls=%fused_computation.30 | convolution fusion | flops 4295229440 | bytes 21495808 | tf_op jit(solution)/shard_map/rd,kde->rke/dot_general | solution.py:76
  288.1 0.8 constant_dynamic-update-slice_fusion
  288.9 3.5 reshape_reshape.3
  292.4 2.0 fusion.52
  295.7 2.3 fusion.30
  298.1 1.6 gather_fusion.5
  299.7 4.3 %all-to-all-start.1 = ((bf16[8,2,64,512]{3,2,1,0:T(8,128)(2,1)}), bf16[8,2,64,512]{3,2,1,0:T(8,128)(2,1)S(1)}, u32[]{:S(2)}, u32[]{:S(2)}) async-start(bf16[8,2,64,512]{3,2,1,0:T(8,128)(2,1)} %bitcast.27), calls=%async_computation.1 | async-start | bytes 2097152 | tf_op jit(solution)/shard_map/all_to_all | solution.py:87
  304.0 15.2 %all-to-all-done.1 = bf16[8,2,64,512]{3,2,1,0:T(8,128)(2,1)S(1)} async-done(((bf16[8,2,64,512]{3,2,1,0:T(8,128)(2,1)}), bf16[8,2,64,512]{3,2,1,0:T(8,128)(2,1)S(1)}, u32[]{:S(2)}, u32[]{:S(2)}) %all-to-all-start.1) | async-done | bytes 1048608 | tf_op jit(solution)/shard_map/all_to_all | solution.py:87
  319.8 8.0 %convolution_convert_fusion = bf16[320,8192]{1,0:T(8,128)(2,1)} fusion(bf16[320,512]{1,0:T(8,128)(2,1)S(1)} %bitcast.130, bf16[512,8192]{1,0:T(8,128)(2,1)} %param.8), kind=kOutput, calls=%fused_computation.8 | convolution fusion | flops 2686976000 | bytes 13959168 | tf_op jit(solution)/shard_map/dot_general | solution.py:90
  327.8 7.7 %reshape.300 = bf16[16,20,8192]{2,1,0:T(8,128)(2,1)} reshape(bf16[320,8192]{1,0:T(8,128)(2,1)} %convolution_convert_fusion) | data formatting | bytes 10485760 | tf_op jit(solution)/shard_map/reshape | solution.py:91
  335.5 80.8 %reduce-scatter.4.cloned.1.call-done = bf16[1,20,8192]{2,1,0:T(8,128)(2,1)} async-done(((bf16[16,20,8192]{2,1,0:T(8,128)(2,1)}), bf16[1,20,8192]{2,1,0:T(8,128)(2,1)}) %reduce-scatter.4.cloned.1.call-update) | async-done | bytes 327696
  (48 shorter events, 5.7 us)
Async XLA Ops:
  6.5 6.7 %copy-start = (bf16[320,512]{1,0:T(8,128)(2,1)S(1)}, bf16[320,512]{1,0:T(8,128)(2,1)}, u32[]{:S(2)}) copy-start(bf16[320,512]{1,0:T(8,128)(2,1)} %param.5) | copy-start | bytes 983044
  6.5 4.5 %copy-start.3 = (s32[40]{0:T(128)S(1)}, s32[40]{0:T(128)}, u32[]{:S(2)}) copy-start(s32[40]{0:T(128)} %param.9) | copy-start | bytes 484
  6.5 57.0 %all-gather.6.cloned.1.call-start = ((), (), s32[]{:S(2)}) async-start(), calls=%async_computation.3 | async-start | bytes 4456448 | tf_op jit(solution)/shard_map/all_gather | solution.py:75
  9.0 107.9 %all-gather.8.cloned.1.call-start = ((), (), s32[]{:S(2)}) async-start(), calls=%async_computation.4 | async-start | bytes 4456448 | tf_op jit(solution)/shard_map/all_gather | solution.py:75
  9.7 160.4 %all-gather.10.cloned.1.call-start = ((), (), s32[]{:S(2)}) async-start(), calls=%async_computation.5 | async-start | bytes 4456448 | tf_op jit(solution)/shard_map/all_gather | solution.py:75
  10.4 212.8 %all-gather.12.cloned.1.call-start = ((), (), s32[]{:S(2)}) async-start(), calls=%async_computation.6 | async-start | bytes 4456448 | tf_op jit(solution)/shard_map/all_gather | solution.py:75
  14.8 19.7 %all-to-all-start = ((bf16[8,2,64,512]{3,2,1,0:T(8,128)(2,1)}), bf16[8,2,64,512]{3,2,1,0:T(8,128)(2,1)S(1)}, u32[]{:S(2)}, u32[]{:S(2)}) async-start(bf16[8,2,64,512]{3,2,1,0:T(8,128)(2,1)} %bitcast.19), calls=%async_computation | async-start | bytes 2097152 | tf_op jit(solution)/shard_map/all_to_all | solution.py:62
  19.2 257.1 %all-gather.14.cloned.1.call-start = ((), (), s32[]{:S(2)}) async-start(), calls=%async_computation.7 | async-start | bytes 4456448 | tf_op jit(solution)/shard_map/all_gather | solution.py:75
  294.4 1.3 copy-start.2
  299.7 19.5 %all-to-all-start.1 = ((bf16[8,2,64,512]{3,2,1,0:T(8,128)(2,1)}), bf16[8,2,64,512]{3,2,1,0:T(8,128)(2,1)S(1)}, u32[]{:S(2)}, u32[]{:S(2)}) async-start(bf16[8,2,64,512]{3,2,1,0:T(8,128)(2,1)} %bitcast.27), calls=%async_computation.1 | async-start | bytes 2097152 | tf_op jit(solution)/shard_map/all_to_all | solution.py:87
  304.0 112.3 %reduce-scatter.4.cloned.1.call-start = ((), (), s32[]{:S(2)}) async-start(), calls=%async_computation.8 | async-start | bytes 6684672
  335.5 80.8 %copy-start.1 = (bf16[320,512]{1,0:T(8,128)(2,1)S(1)}, bf16[320,512]{1,0:T(8,128)(2,1)}, u32[]{:S(2)}) copy-start(bf16[320,512]{1,0:T(8,128)(2,1)} %param.5) | copy-start | bytes 983044
Sparse Core Ops, SparseCore 0:
  9.5 54.0 all-gather.5
  65.7 51.0 all-gather.7
  119.0 51.0 all-gather.9
  172.1 51.0 all-gather.11
  225.2 51.0 all-gather.13
  335.7 80.5 reduce-scatter.3

commit v2 on v1

--- a/solution.py
+++ b/solution.py
@@ -11,7 +11,7 @@
 CH_DEV = 5
 CAPC = 5
 KEYS = 256
-ROW_CHUNKS = 5
+ROW_CHUNKS = 1
 
 
 def attend(query_block, keys, values):

time: 424 us -> 308 us (0.73)
  waiting for transfers between devices: 304 us -> 224 us
  matrix products: 68.7 us -> 39 us
  local copies, waits for them, and re-layouts: 26.9 us -> 20.8 us
    all_gather x5 -> x1, waiting for transfers between devices: 192 us -> 114 us  [on_device(): rows = lax.all_gather(nb_chunks[i], 'tensor', axis=0, tiled=True)]
    dot_general x5 -> x1, matrix products: 57.8 us -> 28.1 us  [on_device(): jnp.einsum('rd,kde->rke', rows, kv_weight, preferred_element_type=jnp.flo...]
    unnamed x7 -> x3, waiting for transfers between devices: 83.2 us -> 81.3 us
  transfers between devices with their start and end apart: 8 -> 4, of which waited for: 8 -> 4; matrix products, arithmetic and copies ran while one was open for 13% -> 2% of each run, Pallas kernels for 0% -> 0%
where the time goes in v2:
time: 308 us
  waiting for transfers between devices  224 us (73%)
  matrix products  39 us (13%)
  local copies, waits for them, and re-layouts  20.8 us (7%)
  between operations  13.5 us (4%)
  starting transfers between devices  8.7 us (3%)
    all_gather x1, waiting for transfers between devices, on_device(): rows = lax.all_gather(nb_chunks[i], 'tensor', axis=0, tiled=True)  114 us
    unnamed x3, waiting for transfers between devices  81.3 us
    dot_general x1, matrix products, on_device(): jnp.einsum('rd,kde->rke', rows, kv_weight, preferred_element_type=jnp.flo...  28.1 us
    all_to_all x1, waiting for transfers between devices, on_device(): lax.all_to_all(send_a, ('section', 'seq'), split_axis=0, concat_axis=0, t...  15.2 us
    all_to_all x1, waiting for transfers between devices, on_device(): lax.all_to_all(send_q, ('section', 'seq'), split_axis=0, concat_axis=0, t...  13.9 us
    dot_general x1, matrix products, on_device(): jnp.dot(attended_flat, out_weight, preferred_element_type=jnp.float32)  8.05 us
    reshape x1, local copies, waits for them, and re-layouts, on_device(): partial.astype(jnp.bfloat16).reshape(tensor_size, -1, out_weight.shape[1])  7.77 us
  transfers between devices with their start and end apart: 4, of which 4 were waited for; matrix products, arithmetic and copies ran while one was open for 2% of the time, Pallas kernels for 0%

profile of v2, /device:TPU:0, one launch (start us, length us, event | category | flops | bytes accessed | tf_op | source)
XLA Modules:
  0.0 307.6 jit_solution(17804573465691138894)
XLA Ops:
  6.5 0.7 all-gather.2.cloned.1.call-update
  7.3 0.6 gather_fusion
  8.0 0.2 convert_reduce_fusion
  8.2 0.7 gather_fusion.1
  9.0 0.1 fusion.15
  9.1 0.1 copy.23
  9.1 0.1 reshape.309
  9.2 1.6 gather_fusion.2
  10.8 4.4 %all-to-all-start = ((bf16[8,2,64,512]{3,2,1,0:T(8,128)(2,1)}), bf16[8,2,64,512]{3,2,1,0:T(8,128)(2,1)S(1)}, u32[]{:S(2)}, u32[]{:S(2)}) async-start(bf16[8,2,64,512]{3,2,1,0:T(8,128)(2,1)} %bitcast.5), calls=%async_computation | async-start | bytes 2097152 | tf_op jit(solution)/shard_map/all_to_all | solution.py:62
  15.2 0.2 select_reduce_fusion
  15.4 0.6 gather_fusion.3
  16.1 0.1 iota_compare_fusion.1
  16.3 0.1 fusion.16
  16.4 0.1 copy.27
  16.4 0.1 reshape.331
  16.6 13.9 %all-to-all-done = bf16[8,2,64,512]{3,2,1,0:T(8,128)(2,1)S(1)} async-done(((bf16[8,2,64,512]{3,2,1,0:T(8,128)(2,1)}), bf16[8,2,64,512]{3,2,1,0:T(8,128)(2,1)S(1)}, u32[]{:S(2)}, u32[]{:S(2)}) %all-to-all-start) | async-done | bytes 1048608 | tf_op jit(solution)/shard_map/all_to_all | solution.py:62
  30.5 0.6 gather_fusion.4
  31.1 113.7 %all-gather.2.cloned.1.call-done = bf16[1280,8192]{1,0:T(8,128)(2,1)} async-done(((bf16[80,8192]{1,0:T(8,128)(2,1)}), bf16[1280,8192]{1,0:T(8,128)(2,1)}) %all-gather.2.cloned.1.call-update) | async-done | bytes 20971536 | tf_op jit(solution)/shard_map/all_gather | solution.py:75
  144.8 28.1 %fusion.3 = bf16[1280,2,512]{2,0,1:T(8,128)(2,1)} fusion(bf16[2,8192,512]{2,1,0:T(8,128)(2,1)} %param.7, bf16[1280,8192]{1,0:T(8,128)(2,1)} %all-gather.2.cloned.1.call-done), kind=kOutput, calls=%fused_computation.11 | convolution fusion | flops 21476147200 | bytes 40370176 | tf_op jit(solution)/shard_map/rd,kde->rke/dot_general | solution.py:76
  172.8 3.5 %reshape_reshape_stack_reshape.3 = bf16[5,256,2,4,128]{4,3,1,0,2:T(4,128)(2,1)S(1)} reshape(bf16[1280,2,512]{2,0,1:T(8,128)(2,1)} %fusion.3) | data formatting | bytes 5242880 | tf_op jit(solution)/shard_map/reshape;reshape;stack;reshape | solution.py:79
  176.4 2.0 fusion.32
  178.3 0.6 convolution_multiply_fusion
  178.9 0.4 fusion.33
  179.4 0.9 copy-done.2
  180.3 2.3 fusion.10
  182.6 1.6 gather_fusion.5
  184.2 4.3 %all-to-all-start.1 = ((bf16[8,2,64,512]{3,2,1,0:T(8,128)(2,1)}), bf16[8,2,64,512]{3,2,1,0:T(8,128)(2,1)S(1)}, u32[]{:S(2)}, u32[]{:S(2)}) async-start(bf16[8,2,64,512]{3,2,1,0:T(8,128)(2,1)} %bitcast.13), calls=%async_computation.1 | async-start | bytes 2097152 | tf_op jit(solution)/shard_map/all_to_all | solution.py:87
  188.6 15.2 %all-to-all-done.1 = bf16[8,2,64,512]{3,2,1,0:T(8,128)(2,1)S(1)} async-done(((bf16[8,2,64,512]{3,2,1,0:T(8,128)(2,1)}), bf16[8,2,64,512]{3,2,1,0:T(8,128)(2,1)S(1)}, u32[]{:S(2)}, u32[]{:S(2)}) %all-to-all-start.1) | async-done | bytes 1048608 | tf_op jit(solution)/shard_map/all_to_all | solution.py:87
  203.7 0.6 gather_fusion.6
  204.3 8.0 %convolution_convert_fusion = bf16[320,8192]{1,0:T(8,128)(2,1)} fusion(bf16[320,512]{1,0:T(8,128)(2,1)S(1)} %bitcast.84, bf16[512,8192]{1,0:T(8,128)(2,1)} %param.8), kind=kOutput, calls=%fused_computation.10 | convolution fusion | flops 2686976000 | bytes 13959168 | tf_op jit(solution)/shard_map/dot_general | solution.py:90
  212.4 7.8 %reshape.289 = bf16[16,20,8192]{2,1,0:T(8,128)(2,1)} reshape(bf16[320,8192]{1,0:T(8,128)(2,1)} %convolution_convert_fusion) | data formatting | bytes 10485760 | tf_op jit(solution)/shard_map/reshape | solution.py:91
  220.2 80.6 %reduce-scatter.4.cloned.1.call-done = bf16[1,20,8192]{2,1,0:T(8,128)(2,1)} async-done(((bf16[16,20,8192]{2,1,0:T(8,128)(2,1)}), bf16[1,20,8192]{2,1,0:T(8,128)(2,1)}) %reduce-scatter.4.cloned.1.call-update) | async-done | bytes 327696
  (27 shorter events, 0.5 us)
Async XLA Ops:
  6.5 2.7 copy-start
  6.5 0.8 copy-start.3
  6.5 138.2 %all-gather.2.cloned.1.call-start = ((), (), s32[]{:S(2)}) async-start(), calls=%async_computation.3 | async-start | bytes 22282240 | tf_op jit(solution)/shard_map/all_gather | solution.py:75
  10.8 19.7 %all-to-all-start = ((bf16[8,2,64,512]{3,2,1,0:T(8,128)(2,1)}), bf16[8,2,64,512]{3,2,1,0:T(8,128)(2,1)S(1)}, u32[]{:S(2)}, u32[]{:S(2)}) async-start(bf16[8,2,64,512]{3,2,1,0:T(8,128)(2,1)} %bitcast.5), calls=%async_computation | async-start | bytes 2097152 | tf_op jit(solution)/shard_map/all_to_all | solution.py:62
  178.9 1.3 copy-start.2
  184.2 19.5 %all-to-all-start.1 = ((bf16[8,2,64,512]{3,2,1,0:T(8,128)(2,1)}), bf16[8,2,64,512]{3,2,1,0:T(8,128)(2,1)S(1)}, u32[]{:S(2)}, u32[]{:S(2)}) async-start(bf16[8,2,64,512]{3,2,1,0:T(8,128)(2,1)} %bitcast.13), calls=%async_computation.1 | async-start | bytes 2097152 | tf_op jit(solution)/shard_map/all_to_all | solution.py:87
  188.5 112.2 %reduce-scatter.4.cloned.1.call-start = ((), (), s32[]{:S(2)}) async-start(), calls=%async_computation.4 | async-start | bytes 6684672
  220.2 80.6 %copy-start.1 = (bf16[320,512]{1,0:T(8,128)(2,1)S(1)}, bf16[320,512]{1,0:T(8,128)(2,1)}, u32[]{:S(2)}) copy-start(bf16[320,512]{1,0:T(8,128)(2,1)} %param.5) | copy-start | bytes 983044
Sparse Core Ops, SparseCore 0:
  9.5 135.2 all-gather.1
  220.3 80.3 reduce-scatter.3

commit v3 on v2

--- a/solution.py
+++ b/solution.py
@@ -85,10 +85,11 @@
     )
     send_a = attended[send_a_idx]
     recv_a = lax.all_to_all(send_a, ("section", "seq"), split_axis=0, concat_axis=0, tiled=True)
-    attended_flat = recv_a[own_owner, own_arrival].reshape(CH_DEV * SPAN, cols)
+    attended_rows = recv_a[own_owner, own_arrival].reshape(tensor_size, -1, cols)
 
-    partial = jnp.dot(attended_flat, out_weight, preferred_element_type=jnp.float32)
-    partial = partial.astype(jnp.bfloat16).reshape(tensor_size, -1, out_weight.shape[1])
+    partial = jnp.einsum(
+        "srk,kn->srn", attended_rows, out_weight, preferred_element_type=jnp.float32
+    ).astype(jnp.bfloat16)
     mixed = lax.psum_scatter(partial, "tensor", scatter_dimension=0, tiled=True)
     return mixed.reshape(-1, out_weight.shape[1])
 

time: 308 us -> 301 us (0.977)
  local copies, waits for them, and re-layouts: 20.8 us -> 13.1 us
    reshape x1, local copies, waits for them, and re-layouts: 7.77 us -> 0.07 us  [on_device(): recv_a[own_owner, own_arrival].reshape(tensor_size, -1, cols)]
where the time goes in v3:
time: 301 us; the launch traced here: 300 us
  waiting for transfers between devices  224 us (74%)
  matrix products  39.7 us (13%)
  between operations  13.6 us (5%)
  local copies, waits for them, and re-layouts  13.1 us (4%)
  starting transfers between devices  8.7 us (3%)
    all_gather x1, waiting for transfers between devices, on_device(): rows = lax.all_gather(nb_chunks[i], 'tensor', axis=0, tiled=True)  114 us
    unnamed x3, waiting for transfers between devices  81.1 us
    dot_general x1, matrix products, on_device(): jnp.einsum('rd,kde->rke', rows, kv_weight, preferred_element_type=jnp.flo...  28.1 us
    all_to_all x1, waiting for transfers between devices, on_device(): lax.all_to_all(send_a, ('section', 'seq'), split_axis=0, concat_axis=0, t...  15.2 us
    all_to_all x1, waiting for transfers between devices, on_device(): lax.all_to_all(send_q, ('section', 'seq'), split_axis=0, concat_axis=0, t...  13.9 us
    dot_general x1, matrix products, on_device(): jnp.einsum('srk,kn->srn', attended_rows, out_weight, preferred_element_ty...  8.73 us
  transfers between devices with their start and end apart: 4, of which 4 were waited for; matrix products, arithmetic and copies ran while one was open for 2% of the time, Pallas kernels for 0%

profile of v3, /device:TPU:0, one launch (start us, length us, event | category | flops | bytes accessed | tf_op | source)
XLA Modules:
  0.0 300.4 jit_solution(7362749550888203316)
XLA Ops:
  6.5 0.7 all-gather.2.cloned.1.call-update
  7.3 0.6 gather_fusion
  8.0 0.2 convert_reduce_fusion
  8.2 0.7 gather_fusion.1
  8.8 0.1 iota_compare_fusion.3
  9.0 0.1 fusion.16
  9.1 0.1 copy.23
  9.1 0.1 reshape.305
  9.2 1.6 gather_fusion.2
  10.8 4.4 %all-to-all-start = ((bf16[8,2,64,512]{3,2,1,0:T(8,128)(2,1)}), bf16[8,2,64,512]{3,2,1,0:T(8,128)(2,1)S(1)}, u32[]{:S(2)}, u32[]{:S(2)}) async-start(bf16[8,2,64,512]{3,2,1,0:T(8,128)(2,1)} %bitcast.5), calls=%async_computation | async-start | bytes 2097152 | tf_op jit(solution)/shard_map/all_to_all | solution.py:62
  15.2 0.2 select_reduce_fusion
  15.4 0.6 gather_fusion.3
  16.1 0.1 iota_compare_fusion.1
  16.3 0.1 fusion.17
  16.4 0.1 copy.27
  16.4 0.1 reshape.327
  16.6 13.9 %all-to-all-done = bf16[8,2,64,512]{3,2,1,0:T(8,128)(2,1)S(1)} async-done(((bf16[8,2,64,512]{3,2,1,0:T(8,128)(2,1)}), bf16[8,2,64,512]{3,2,1,0:T(8,128)(2,1)S(1)}, u32[]{:S(2)}, u32[]{:S(2)}) %all-to-all-start) | async-done | bytes 1048608 | tf_op jit(solution)/shard_map/all_to_all | solution.py:62
  30.5 0.6 gather_fusion.4
  31.1 113.7 %all-gather.2.cloned.1.call-done = bf16[1280,8192]{1,0:T(8,128)(2,1)} async-done(((bf16[80,8192]{1,0:T(8,128)(2,1)}), bf16[1280,8192]{1,0:T(8,128)(2,1)}) %all-gather.2.cloned.1.call-update) | async-done | bytes 20971536 | tf_op jit(solution)/shard_map/all_gather | solution.py:75
  144.8 28.1 %fusion.4 = bf16[1280,2,512]{2,0,1:T(8,128)(2,1)} fusion(bf16[2,8192,512]{2,1,0:T(8,128)(2,1)} %param.7, bf16[1280,8192]{1,0:T(8,128)(2,1)} %all-gather.2.cloned.1.call-done), kind=kOutput, calls=%fused_computation.12 | convolution fusion | flops 21476147200 | bytes 40370176 | tf_op jit(solution)/shard_map/rd,kde->rke/dot_general | solution.py:76
  172.8 3.5 %reshape_reshape_stack_reshape.3 = bf16[5,256,2,4,128]{4,3,1,0,2:T(4,128)(2,1)S(1)} reshape(bf16[1280,2,512]{2,0,1:T(8,128)(2,1)} %fusion.4) | data formatting | bytes 5242880 | tf_op jit(solution)/shard_map/reshape;reshape;stack;reshape | solution.py:79
  176.4 2.0 fusion.33
  178.3 0.6 convolution_multiply_fusion
  178.9 0.4 fusion.34
  179.4 0.9 copy-done.2
  180.3 2.3 fusion.11
  182.6 1.6 gather_fusion.5
  184.2 4.3 %all-to-all-start.1 = ((bf16[8,2,64,512]{3,2,1,0:T(8,128)(2,1)}), bf16[8,2,64,512]{3,2,1,0:T(8,128)(2,1)S(1)}, u32[]{:S(2)}, u32[]{:S(2)}) async-start(bf16[8,2,64,512]{3,2,1,0:T(8,128)(2,1)} %bitcast.13), calls=%async_computation.1 | async-start | bytes 2097152 | tf_op jit(solution)/shard_map/all_to_all | solution.py:87
  188.6 15.2 %all-to-all-done.1 = bf16[8,2,64,512]{3,2,1,0:T(8,128)(2,1)S(1)} async-done(((bf16[8,2,64,512]{3,2,1,0:T(8,128)(2,1)}), bf16[8,2,64,512]{3,2,1,0:T(8,128)(2,1)S(1)}, u32[]{:S(2)}, u32[]{:S(2)}) %all-to-all-start.1) | async-done | bytes 1048608 | tf_op jit(solution)/shard_map/all_to_all | solution.py:87
  203.7 0.6 gather_fusion.6
  204.4 8.7 %convolution_convert_fusion = bf16[16,20,8192]{2,1,0:T(8,128)(2,1)} fusion(bf16[16,20,512]{2,1,0:T(8,128)(2,1)S(1)} %reshape.285, bf16[512,8192]{1,0:T(8,128)(2,1)} %param.8), kind=kOutput, calls=%fused_computation.10 | convolution fusion | flops 2686976000 | bytes 13959168 | tf_op jit(solution)/shard_map/srk,kn->srn/dot_general | solution.py:90
  213.2 80.4 %reduce-scatter.4.cloned.1.call-done = bf16[1,20,8192]{2,1,0:T(8,128)(2,1)} async-done(((bf16[16,20,8192]{2,1,0:T(8,128)(2,1)}), bf16[1,20,8192]{2,1,0:T(8,128)(2,1)}) %reduce-scatter.4.cloned.1.call-update) | async-done | bytes 327696
  (27 shorter events, 0.5 us)
Async XLA Ops:
  6.5 2.7 copy-start
  6.5 0.8 copy-start.3
  6.5 138.2 %all-gather.2.cloned.1.call-start = ((), (), s32[]{:S(2)}) async-start(), calls=%async_computation.3 | async-start | bytes 22282240 | tf_op jit(solution)/shard_map/all_gather | solution.py:75
  10.8 19.7 %all-to-all-start = ((bf16[8,2,64,512]{3,2,1,0:T(8,128)(2,1)}), bf16[8,2,64,512]{3,2,1,0:T(8,128)(2,1)S(1)}, u32[]{:S(2)}, u32[]{:S(2)}) async-start(bf16[8,2,64,512]{3,2,1,0:T(8,128)(2,1)} %bitcast.5), calls=%async_computation | async-start | bytes 2097152 | tf_op jit(solution)/shard_map/all_to_all | solution.py:62
  178.9 1.3 copy-start.2
  184.2 19.5 %all-to-all-start.1 = ((bf16[8,2,64,512]{3,2,1,0:T(8,128)(2,1)}), bf16[8,2,64,512]{3,2,1,0:T(8,128)(2,1)S(1)}, u32[]{:S(2)}, u32[]{:S(2)}) async-start(bf16[8,2,64,512]{3,2,1,0:T(8,128)(2,1)} %bitcast.13), calls=%async_computation.1 | async-start | bytes 2097152 | tf_op jit(solution)/shard_map/all_to_all | solution.py:87
  188.5 105.1 %reduce-scatter.4.cloned.1.call-start = ((), (), s32[]{:S(2)}) async-start(), calls=%async_computation.4 | async-start | bytes 6684672
  213.1 80.4 %copy-start.1 = (bf16[320,512]{1,0:T(8,128)(2,1)S(1)}, bf16[320,512]{1,0:T(8,128)(2,1)}, u32[]{:S(2)}) copy-start(bf16[320,512]{1,0:T(8,128)(2,1)} %param.5) | copy-start | bytes 983044
Sparse Core Ops, SparseCore 0:
  9.5 135.2 all-gather.1
  213.3 80.2 reduce-scatter.3

commit v4 on v3

--- a/solution.py
+++ b/solution.py
@@ -11,7 +11,6 @@
 CH_DEV = 5
 CAPC = 5
 KEYS = 256
-ROW_CHUNKS = 1
 
 
 def attend(query_block, keys, values):
@@ -68,16 +67,13 @@
     slot_place = arrival[slot_span]
     q_for_slot = recv_q[slot_group, slot_place].reshape(CAPC, SPAN, heads_local, HD)
 
-    sub = rows_local // ROW_CHUNKS
-    nb_chunks = neighbours.reshape(ROW_CHUNKS, sub, neighbours.shape[1])
-    kv_parts = []
-    for i in range(ROW_CHUNKS):
-        rows = lax.all_gather(nb_chunks[i], "tensor", axis=0, tiled=True)
-        part = jnp.einsum("rd,kde->rke", rows, kv_weight, preferred_element_type=jnp.float32)
-        kv_parts.append(part.astype(jnp.bfloat16).reshape(tensor_size, sub, 2, cols))
-    kv = jnp.stack(kv_parts, axis=1).reshape(tensor_size * rows_local, 2, cols)
-    kv = kv.reshape(CAPC, KEYS, 2, heads_local, HD)
-    attended = attend(q_for_slot, kv[:, :, 0], kv[:, :, 1]).reshape(CAPC, SPAN, cols)
+    rows = lax.all_gather(neighbours, "tensor", axis=0, tiled=True)
+    rows = rows.reshape(CAPC, KEYS, rows.shape[1])
+    keys = jnp.einsum("skd,de->ske", rows, kv_weight[0], preferred_element_type=jnp.float32)
+    values = jnp.einsum("skd,de->ske", rows, kv_weight[1], preferred_element_type=jnp.float32)
+    keys = keys.astype(jnp.bfloat16).reshape(CAPC, KEYS, heads_local, HD)
+    values = values.astype(jnp.bfloat16).reshape(CAPC, KEYS, heads_local, HD)
+    attended = attend(q_for_slot, keys, values).reshape(CAPC, SPAN, cols)
 
     pick_a = (slot_group[None, None, :] == peer_ids) & (slot_place[None, None, :] == place_ids)
     send_a_idx = jnp.sum(

time: 301 us -> 304 us (level)
  matrix products: 39.7 us -> 48.8 us
  local copies, waits for them, and re-layouts: 13.1 us -> 6.74 us
    dot_general x1 -> x2, matrix products: 28.1 us -> 35.9 us  [the longest x1 18.4 us: on_device(): jnp.einsum('skd,de->ske', rows, kv_weight[1], preferred_element_type=jnp....]
    another operation x1 -> x0, local copies, waits for them, and re-layouts: 3.54 us -> none  [on_device(): kv = kv.reshape(CAPC, KEYS, 2, heads_local, HD)]
where the time goes in v4:
time: 304 us
  waiting for transfers between devices  224 us (74%)
  matrix products  48.8 us (16%)
  between operations  13.5 us (4%)
  starting transfers between devices  8.71 us (3%)
  local copies, waits for them, and re-layouts  6.74 us (2%)
    all_gather x1, waiting for transfers between devices, on_device(): rows = lax.all_gather(neighbours, 'tensor', axis=0, tiled=True)  114 us
    unnamed x3, waiting for transfers between devices  81.6 us
    dot_general x1, matrix products, on_device(): jnp.einsum('skd,de->ske', rows, kv_weight[1], preferred_element_type=jnp....  18.4 us
    dot_general x1, matrix products, on_device(): jnp.einsum('skd,de->ske', rows, kv_weight[0], preferred_element_type=jnp....  17.5 us
    all_to_all x1, waiting for transfers between devices, on_device(): lax.all_to_all(send_a, ('section', 'seq'), split_axis=0, concat_axis=0, t...  15.2 us
    all_to_all x1, waiting for transfers between devices, on_device(): lax.all_to_all(send_q, ('section', 'seq'), split_axis=0, concat_axis=0, t...  13.9 us
    dot_general x1, matrix products, on_device(): jnp.einsum('srk,kn->srn', attended_rows, out_weight, preferred_element_ty...  8.77 us
  transfers between devices with their start and end apart: 4, of which 4 were waited for; matrix products, arithmetic and copies ran while one was open for 2% of the time, Pallas kernels for 0%

profile of v4, /device:TPU:0, one launch (start us, length us, event | category | flops | bytes accessed | tf_op | source)
XLA Modules:
  0.0 303.6 jit_solution(3251046413988377283)
XLA Ops:
  6.5 0.7 all-gather.2.cloned.1.call-update
  7.3 0.6 gather_fusion
  8.0 0.2 convert_reduce_fusion
  8.2 0.7 gather_fusion.1
  8.8 0.1 iota_compare_fusion.3
  8.9 0.1 iota_compare_fusion.4
  9.0 0.1 fusion.37
  9.1 0.1 copy.22
  9.1 0.1 reshape.317
  9.2 1.6 gather_fusion.2
  10.8 4.4 %all-to-all-start = ((bf16[8,2,64,512]{3,2,1,0:T(8,128)(2,1)}), bf16[8,2,64,512]{3,2,1,0:T(8,128)(2,1)S(1)}, u32[]{:S(2)}, u32[]{:S(2)}) async-start(bf16[8,2,64,512]{3,2,1,0:T(8,128)(2,1)} %bitcast.6), calls=%async_computation | async-start | bytes 2097152 | tf_op jit(solution)/shard_map/all_to_all | solution.py:61
  15.2 0.2 select_reduce_fusion
  15.4 0.6 gather_fusion.3
  16.1 0.1 iota_compare_fusion.1
  16.2 0.1 iota_compare_fusion.2
  16.3 0.1 fusion.38
  16.4 0.1 copy.27
  16.4 0.1 reshape.339
  16.6 13.9 %all-to-all-done = bf16[8,2,64,512]{3,2,1,0:T(8,128)(2,1)S(1)} async-done(((bf16[8,2,64,512]{3,2,1,0:T(8,128)(2,1)}), bf16[8,2,64,512]{3,2,1,0:T(8,128)(2,1)S(1)}, u32[]{:S(2)}, u32[]{:S(2)}) %all-to-all-start) | async-done | bytes 1048608 | tf_op jit(solution)/shard_map/all_to_all | solution.py:61
  30.5 0.6 gather_fusion.4
  31.1 113.7 %all-gather.2.cloned.1.call-done = bf16[1280,8192]{1,0:T(8,128)(2,1)} async-done(((bf16[80,8192]{1,0:T(8,128)(2,1)}), bf16[1280,8192]{1,0:T(8,128)(2,1)}) %all-gather.2.cloned.1.call-update) | async-done | bytes 20971536 | tf_op jit(solution)/shard_map/all_gather | solution.py:70
  144.8 18.4 %fusion.18 = bf16[5,32,4,8,128]{4,3,2,1,0:T(8,128)(2,1)} fusion(bf16[5,256,8192]{2,1,0:T(8,128)(2,1)} %bitcast.100, bf16[2,8192,512]{2,1,0:T(8,128)(2,1)} %param.7), kind=kOutput, calls=%fused_computation.20 | convolution fusion | flops 10738073600 | bytes 30670848 | tf_op jit(solution)/shard_map/skd,de->ske/dot_general | solution.py:73
  163.1 17.5 %fusion.15 = bf16[5,32,4,8,128]{4,3,2,1,0:T(8,128)(2,1)S(1)} fusion(bf16[5,256,8192]{2,1,0:T(8,128)(2,1)} %bitcast.101, bf16[2,8192,512]{2,1,0:T(8,128)(2,1)} %param.7), kind=kOutput, calls=%fused_computation.19 | convolution fusion | flops 10738073600 | bytes 30670848 | tf_op jit(solution)/shard_map/skd,de->ske/dot_general | solution.py:72
  180.7 0.6 convolution_multiply_fusion
  181.2 0.4 fusion.54
  181.7 3.6 %fusion.30 = bf16[5,4,8,8,128]{4,3,2,1,0:T(8,128)(2,1)S(1)} fusion(bf16[5,32,4,8,128]{4,3,2,1,0:T(8,128)(2,1)} %fusion.18, f32[5,4,64]{2,1,0:T(4,128)S(1)} %fusion.54, f32[5,4,64,256]{3,2,1,0:T(8,128)S(1)} %convolution_multiply_fusion), kind=kOutput, calls=%fused_computation.30 | convolution fusion | flops 85034496 | bytes 2954240 | tf_op jit(solution)/shard_map/bhqk,bkhd->bqhd/dot_general | solution.py:24
  185.4 1.6 gather_fusion.5
  187.0 4.3 %all-to-all-start.1 = ((bf16[8,2,64,512]{3,2,1,0:T(8,128)(2,1)}), bf16[8,2,64,512]{3,2,1,0:T(8,128)(2,1)S(1)}, u32[]{:S(2)}, u32[]{:S(2)}) async-start(bf16[8,2,64,512]{3,2,1,0:T(8,128)(2,1)} %bitcast.15), calls=%async_computation.1 | async-start | bytes 2097152 | tf_op jit(solution)/shard_map/all_to_all | solution.py:83
  191.3 15.2 %all-to-all-done.1 = bf16[8,2,64,512]{3,2,1,0:T(8,128)(2,1)S(1)} async-done(((bf16[8,2,64,512]{3,2,1,0:T(8,128)(2,1)}), bf16[8,2,64,512]{3,2,1,0:T(8,128)(2,1)S(1)}, u32[]{:S(2)}, u32[]{:S(2)}) %all-to-all-start.1) | async-done | bytes 1048608 | tf_op jit(solution)/shard_map/all_to_all | solution.py:83
  206.5 0.6 gather_fusion.6
  207.1 8.8 %convolution_convert_fusion = bf16[16,20,8192]{2,1,0:T(8,128)(2,1)} fusion(bf16[16,20,512]{2,1,0:T(8,128)(2,1)S(1)} %reshape.297, bf16[512,8192]{1,0:T(8,128)(2,1)} %param.8), kind=kOutput, calls=%fused_computation.8 | convolution fusion | flops 2686976000 | bytes 13959168 | tf_op jit(solution)/shard_map/srk,kn->srn/dot_general | solution.py:86
  215.9 80.8 %reduce-scatter.4.cloned.1.call-done = bf16[1,20,8192]{2,1,0:T(8,128)(2,1)} async-done(((bf16[16,20,8192]{2,1,0:T(8,128)(2,1)}), bf16[1,20,8192]{2,1,0:T(8,128)(2,1)}) %reduce-scatter.4.cloned.1.call-update) | async-done | bytes 327696
  (22 shorter events, 0.3 us)
Async XLA Ops:
  6.5 2.7 copy-start
  6.5 0.8 copy-start.1
  6.5 138.2 %all-gather.2.cloned.1.call-start = ((), (), s32[]{:S(2)}) async-start(), calls=%async_computation.3 | async-start | bytes 22282240 | tf_op jit(solution)/shard_map/all_gather | solution.py:70
  10.8 19.7 %all-to-all-start = ((bf16[8,2,64,512]{3,2,1,0:T(8,128)(2,1)}), bf16[8,2,64,512]{3,2,1,0:T(8,128)(2,1)S(1)}, u32[]{:S(2)}, u32[]{:S(2)}) async-start(bf16[8,2,64,512]{3,2,1,0:T(8,128)(2,1)} %bitcast.6), calls=%async_computation | async-start | bytes 2097152 | tf_op jit(solution)/shard_map/all_to_all | solution.py:61
  187.0 19.5 %all-to-all-start.1 = ((bf16[8,2,64,512]{3,2,1,0:T(8,128)(2,1)}), bf16[8,2,64,512]{3,2,1,0:T(8,128)(2,1)S(1)}, u32[]{:S(2)}, u32[]{:S(2)}) async-start(bf16[8,2,64,512]{3,2,1,0:T(8,128)(2,1)} %bitcast.15), calls=%async_computation.1 | async-start | bytes 2097152 | tf_op jit(solution)/shard_map/all_to_all | solution.py:83
  191.2 105.5 %reduce-scatter.4.cloned.1.call-start = ((), (), s32[]{:S(2)}) async-start(), calls=%async_computation.4 | async-start | bytes 6684672
Sparse Core Ops, SparseCore 0:
  9.5 135.2 all-gather.1
  216.0 80.6 reduce-scatter.3

commit v5 on v4

--- a/solution.py
+++ b/solution.py
@@ -69,10 +69,9 @@
 
     rows = lax.all_gather(neighbours, "tensor", axis=0, tiled=True)
     rows = rows.reshape(CAPC, KEYS, rows.shape[1])
-    keys = jnp.einsum("skd,de->ske", rows, kv_weight[0], preferred_element_type=jnp.float32)
-    values = jnp.einsum("skd,de->ske", rows, kv_weight[1], preferred_element_type=jnp.float32)
-    keys = keys.astype(jnp.bfloat16).reshape(CAPC, KEYS, heads_local, HD)
-    values = values.astype(jnp.bfloat16).reshape(CAPC, KEYS, heads_local, HD)
+    kv = jnp.einsum("skd,cde->cske", rows, kv_weight, preferred_element_type=jnp.float32)
+    kv = kv.astype(jnp.bfloat16).reshape(2, CAPC, KEYS, heads_local, HD)
+    keys, values = kv[0], kv[1]
     attended = attend(q_for_slot, keys, values).reshape(CAPC, SPAN, cols)
 
     pick_a = (slot_group[None, None, :] == peer_ids) & (slot_place[None, None, :] == place_ids)

time: 304 us -> 293 us (0.964)
  matrix products: 48.8 us -> 38.1 us
    dot_general x2 -> x1, matrix products: 35.9 us -> 26.7 us  [on_device(): jnp.einsum('skd,cde->cske', rows, kv_weight, preferred_element_type=jnp.f...]
where the time goes in v5:
time: 293 us
  waiting for transfers between devices  224 us (76%)
  matrix products  38.1 us (13%)
  between operations  13.5 us (5%)
  starting transfers between devices  8.7 us (3%)
  local copies, waits for them, and re-layouts  6.93 us (2%)
    all_gather x1, waiting for transfers between devices, on_device(): rows = lax.all_gather(neighbours, 'tensor', axis=0, tiled=True)  114 us
    unnamed x3, waiting for transfers between devices  81.2 us
    dot_general x1, matrix products, on_device(): jnp.einsum('skd,cde->cske', rows, kv_weight, preferred_element_type=jnp.f...  26.7 us
    all_to_all x1, waiting for transfers between devices, on_device(): lax.all_to_all(send_a, ('section', 'seq'), split_axis=0, concat_axis=0, t...  15.2 us
    all_to_all x1, waiting for transfers between devices, on_device(): lax.all_to_all(send_q, ('section', 'seq'), split_axis=0, concat_axis=0, t...  13.9 us
    dot_general x1, matrix products, on_device(): jnp.einsum('srk,kn->srn', attended_rows, out_weight, preferred_element_ty...  8.77 us
  transfers between devices with their start and end apart: 4, of which 4 were waited for; matrix products, arithmetic and copies ran while one was open for 2% of the time, Pallas kernels for 0%

profile of v5, /device:TPU:0, one launch (start us, length us, event | category | flops | bytes accessed | tf_op | source)
XLA Modules:
  0.0 292.7 jit_solution(11065134920637061341)
XLA Ops:
  6.5 0.7 all-gather.2.cloned.1.call-update
  7.3 0.6 gather_fusion
  8.0 0.2 convert_reduce_fusion
  8.2 0.7 gather_fusion.1
  8.8 0.1 iota_compare_fusion.3
  9.0 0.1 fusion.12
  9.1 0.1 copy.26
  9.1 0.1 reshape.314
  9.2 1.6 gather_fusion.2
  10.8 4.4 %all-to-all-start = ((bf16[8,2,64,512]{3,2,1,0:T(8,128)(2,1)}), bf16[8,2,64,512]{3,2,1,0:T(8,128)(2,1)S(1)}, u32[]{:S(2)}, u32[]{:S(2)}) async-start(bf16[8,2,64,512]{3,2,1,0:T(8,128)(2,1)} %bitcast.8), calls=%async_computation | async-start | bytes 2097152 | tf_op jit(solution)/shard_map/all_to_all | solution.py:61
  15.2 0.2 select_reduce_fusion
  15.4 0.6 gather_fusion.3
  16.1 0.1 iota_compare_fusion.1
  16.2 0.1 iota_compare_fusion.2
  16.3 0.1 fusion.13
  16.4 0.1 copy.31
  16.4 0.1 reshape.336
  16.6 13.9 %all-to-all-done = bf16[8,2,64,512]{3,2,1,0:T(8,128)(2,1)S(1)} async-done(((bf16[8,2,64,512]{3,2,1,0:T(8,128)(2,1)}), bf16[8,2,64,512]{3,2,1,0:T(8,128)(2,1)S(1)}, u32[]{:S(2)}, u32[]{:S(2)}) %all-to-all-start) | async-done | bytes 1048608 | tf_op jit(solution)/shard_map/all_to_all | solution.py:61
  30.5 0.6 gather_fusion.4
  31.1 113.7 %all-gather.2.cloned.1.call-done = bf16[1280,8192]{1,0:T(8,128)(2,1)} async-done(((bf16[80,8192]{1,0:T(8,128)(2,1)}), bf16[1280,8192]{1,0:T(8,128)(2,1)}) %all-gather.2.cloned.1.call-update) | async-done | bytes 20971536 | tf_op jit(solution)/shard_map/all_gather | solution.py:70
  144.8 26.7 %convert_bitcast_fusion = bf16[2,5,256,512]{2,3,1,0:T(8,128)(2,1)S(1)} fusion(bf16[5,256,8192,1]{2,1,0,3:T(8,128)(2,1)} %bitcast.86, bf16[2,8192,512]{2,1,0:T(8,128)(2,1)} %param.7), kind=kOutput, calls=%fused_computation.12 | convolution fusion | flops 21476147200 | bytes 40370176 | tf_op jit(solution)/shard_map/skd,cde->cske/dot_general | solution.py:72
  171.5 0.2 fusion.29
  171.7 0.3 convolution_multiply_fusion
  172.0 0.4 fusion.30
  172.4 2.3 fusion.8
  174.7 0.1 copy.44
  174.8 1.6 gather_fusion.5
  176.4 4.2 %all-to-all-start.1 = ((bf16[8,2,64,512]{3,2,1,0:T(8,128)(2,1)}), bf16[8,2,64,512]{3,2,1,0:T(8,128)(2,1)S(1)}, u32[]{:S(2)}, u32[]{:S(2)}) async-start(bf16[8,2,64,512]{3,2,1,0:T(8,128)(2,1)} %bitcast.16), calls=%async_computation.1 | async-start | bytes 2097152 | tf_op jit(solution)/shard_map/all_to_all | solution.py:82
  180.7 15.2 %all-to-all-done.1 = bf16[8,2,64,512]{3,2,1,0:T(8,128)(2,1)S(1)} async-done(((bf16[8,2,64,512]{3,2,1,0:T(8,128)(2,1)}), bf16[8,2,64,512]{3,2,1,0:T(8,128)(2,1)S(1)}, u32[]{:S(2)}, u32[]{:S(2)}) %all-to-all-start.1) | async-done | bytes 1048608 | tf_op jit(solution)/shard_map/all_to_all | solution.py:82
  195.9 0.6 gather_fusion.6
  196.6 8.8 %convolution_convert_fusion = bf16[16,20,8192]{2,1,0:T(8,128)(2,1)} fusion(bf16[16,20,512]{2,1,0:T(8,128)(2,1)S(1)} %reshape.294, bf16[512,8192]{1,0:T(8,128)(2,1)} %param.8), kind=kOutput, calls=%fused_computation.10 | convolution fusion | flops 2686976000 | bytes 13959168 | tf_op jit(solution)/shard_map/srk,kn->srn/dot_general | solution.py:85
  205.4 80.5 %reduce-scatter.4.cloned.1.call-done = bf16[1,20,8192]{2,1,0:T(8,128)(2,1)} async-done(((bf16[16,20,8192]{2,1,0:T(8,128)(2,1)}), bf16[1,20,8192]{2,1,0:T(8,128)(2,1)}) %reduce-scatter.4.cloned.1.call-update) | async-done | bytes 327696
  (22 shorter events, 0.3 us)
Async XLA Ops:
  6.5 2.7 copy-start
  6.5 0.8 copy-start.1
  6.5 138.2 %all-gather.2.cloned.1.call-start = ((), (), s32[]{:S(2)}) async-start(), calls=%async_computation.3 | async-start | bytes 22282240 | tf_op jit(solution)/shard_map/all_gather | solution.py:70
  10.8 19.7 %all-to-all-start = ((bf16[8,2,64,512]{3,2,1,0:T(8,128)(2,1)}), bf16[8,2,64,512]{3,2,1,0:T(8,128)(2,1)S(1)}, u32[]{:S(2)}, u32[]{:S(2)}) async-start(bf16[8,2,64,512]{3,2,1,0:T(8,128)(2,1)} %bitcast.8), calls=%async_computation | async-start | bytes 2097152 | tf_op jit(solution)/shard_map/all_to_all | solution.py:61
  176.4 19.5 %all-to-all-start.1 = ((bf16[8,2,64,512]{3,2,1,0:T(8,128)(2,1)}), bf16[8,2,64,512]{3,2,1,0:T(8,128)(2,1)S(1)}, u32[]{:S(2)}, u32[]{:S(2)}) async-start(bf16[8,2,64,512]{3,2,1,0:T(8,128)(2,1)} %bitcast.16), calls=%async_computation.1 | async-start | bytes 2097152 | tf_op jit(solution)/shard_map/all_to_all | solution.py:82
  180.7 105.2 %reduce-scatter.4.cloned.1.call-start = ((), (), s32[]{:S(2)}) async-start(), calls=%async_computation.4 | async-start | bytes 6684672
Sparse Core Ops, SparseCore 0:
  9.5 135.2 all-gather.1
  205.5 80.3 reduce-scatter.3

commit v6 on v5

--- a/solution.py
+++ b/solution.py
@@ -85,8 +85,8 @@
     partial = jnp.einsum(
         "srk,kn->srn", attended_rows, out_weight, preferred_element_type=jnp.float32
     ).astype(jnp.bfloat16)
-    mixed = lax.psum_scatter(partial, "tensor", scatter_dimension=0, tiled=True)
-    return mixed.reshape(-1, out_weight.shape[1])
+    pieces = lax.all_to_all(partial, "tensor", split_axis=0, concat_axis=0, tiled=True)
+    return jnp.sum(pieces.astype(jnp.float32), axis=0).astype(jnp.bfloat16)
 
 
 def solution(mesh):

time: 293 us -> 294 us (level)
  waiting for transfers between devices: 224 us -> 144 us
  blocking collectives: 0 us -> 78.9 us
  other arithmetic: 1.38 us -> 6.17 us
    unnamed x3 -> x1, waiting for transfers between devices: 81.2 us -> 0.71 us
    all_to_all x0 -> x1, blocking collectives: none -> 78.9 us  [on_device(): lax.all_to_all(partial, 'tensor', split_axis=0, concat_axis=0, tiled=True)]
    reduce_sum x0 -> x1, other arithmetic: none -> 4.79 us  [on_device(): return jnp.sum(pieces.astype(jnp.float32), axis=0).astype(jnp.bfloat16)]
  transfers between devices with their start and end apart: 4 -> 3, of which waited for: 4 -> 3; matrix products, arithmetic and copies ran while one was open for 2% -> 2% of each run, Pallas kernels for 0% -> 0%
where the time goes in v6:
time: 294 us
  waiting for transfers between devices  144 us (49%)
  blocking collectives  78.9 us (27%)
  matrix products  36.4 us (12%)
  between operations  13.5 us (5%)
  starting transfers between devices  8.66 us (3%)
  local copies, waits for them, and re-layouts  6.93 us (2%)
  other arithmetic  6.17 us (2%)
    all_gather x1, waiting for transfers between devices, on_device(): rows = lax.all_gather(neighbours, 'tensor', axis=0, tiled=True)  114 us
    all_to_all x1, blocking collectives, on_device(): lax.all_to_all(partial, 'tensor', split_axis=0, concat_axis=0, tiled=True)  78.9 us
    dot_general x1, matrix products, on_device(): jnp.einsum('skd,cde->cske', rows, kv_weight, preferred_element_type=jnp.f...  26.7 us
    all_to_all x1, waiting for transfers between devices, on_device(): lax.all_to_all(send_a, ('section', 'seq'), split_axis=0, concat_axis=0, t...  15.2 us
    all_to_all x1, waiting for transfers between devices, on_device(): lax.all_to_all(send_q, ('section', 'seq'), split_axis=0, concat_axis=0, t...  13.9 us
    dot_general x1, matrix products, on_device(): jnp.einsum('srk,kn->srn', attended_rows, out_weight, preferred_element_ty...  7.08 us
  transfers between devices with their start and end apart: 3, of which 3 were waited for; matrix products, arithmetic and copies ran while one was open for 2% of the time, Pallas kernels for 0%

profile of v6, /device:TPU:0, one launch (start us, length us, event | category | flops | bytes accessed | tf_op | source)
XLA Modules:
  0.0 294.2 jit_solution(4807009310627560471)
XLA Ops:
  6.5 0.7 all-gather.2.cloned.1.call-update
  7.3 0.6 gather_fusion
  8.0 0.2 convert_reduce_fusion
  8.2 0.7 gather_fusion.1
  8.8 0.1 iota_compare_fusion.3
  9.0 0.1 fusion.12
  9.1 0.1 copy.19
  9.1 0.1 reshape.310
  9.2 1.6 gather_fusion.2
  10.8 4.4 %all-to-all-start = ((bf16[8,2,64,512]{3,2,1,0:T(8,128)(2,1)}), bf16[8,2,64,512]{3,2,1,0:T(8,128)(2,1)S(1)}, u32[]{:S(2)}, u32[]{:S(2)}) async-start(bf16[8,2,64,512]{3,2,1,0:T(8,128)(2,1)} %bitcast.8), calls=%async_computation | async-start | bytes 2097152 | tf_op jit(solution)/shard_map/all_to_all | solution.py:61
  15.2 0.2 select_reduce_fusion
  15.4 0.6 gather_fusion.3
  16.1 0.1 iota_compare_fusion.1
  16.3 0.1 fusion.13
  16.4 0.1 copy.24
  16.4 0.1 reshape.332
  16.6 13.9 %all-to-all-done = bf16[8,2,64,512]{3,2,1,0:T(8,128)(2,1)S(1)} async-done(((bf16[8,2,64,512]{3,2,1,0:T(8,128)(2,1)}), bf16[8,2,64,512]{3,2,1,0:T(8,128)(2,1)S(1)}, u32[]{:S(2)}, u32[]{:S(2)}) %all-to-all-start) | async-done | bytes 1048608 | tf_op jit(solution)/shard_map/all_to_all | solution.py:61
  30.5 0.6 gather_fusion.4
  31.1 113.7 %all-gather.2.cloned.1.call-done = bf16[1280,8192]{1,0:T(8,128)(2,1)} async-done(((bf16[80,8192]{1,0:T(8,128)(2,1)}), bf16[1280,8192]{1,0:T(8,128)(2,1)}) %all-gather.2.cloned.1.call-update) | async-done | bytes 20971536 | tf_op jit(solution)/shard_map/all_gather | solution.py:70
  144.8 26.7 %convert_bitcast_fusion = bf16[2,5,256,512]{2,3,1,0:T(8,128)(2,1)S(1)} fusion(bf16[5,256,8192,1]{2,1,0,3:T(8,128)(2,1)} %bitcast.84, bf16[2,8192,512]{2,1,0:T(8,128)(2,1)} %param.7), kind=kOutput, calls=%fused_computation.12 | convolution fusion | flops 21476147200 | bytes 40370176 | tf_op jit(solution)/shard_map/skd,cde->cske/dot_general | solution.py:72
  171.5 0.2 fusion.29
  171.7 0.3 convolution_multiply_fusion
  172.0 0.4 fusion.30
  172.4 2.3 fusion.8
  174.7 0.1 copy.37
  174.8 1.6 gather_fusion.5
  176.4 4.2 %all-to-all-start.1 = ((bf16[8,2,64,512]{3,2,1,0:T(8,128)(2,1)}), bf16[8,2,64,512]{3,2,1,0:T(8,128)(2,1)S(1)}, u32[]{:S(2)}, u32[]{:S(2)}) async-start(bf16[8,2,64,512]{3,2,1,0:T(8,128)(2,1)} %bitcast.16), calls=%async_computation.1 | async-start | bytes 2097152 | tf_op jit(solution)/shard_map/all_to_all | solution.py:82
  180.7 15.2 %all-to-all-done.1 = bf16[8,2,64,512]{3,2,1,0:T(8,128)(2,1)S(1)} async-done(((bf16[8,2,64,512]{3,2,1,0:T(8,128)(2,1)}), bf16[8,2,64,512]{3,2,1,0:T(8,128)(2,1)S(1)}, u32[]{:S(2)}, u32[]{:S(2)}) %all-to-all-start.1) | async-done | bytes 1048608 | tf_op jit(solution)/shard_map/all_to_all | solution.py:82
  195.9 0.6 gather_fusion.6
  196.6 7.1 %convolution_convert_fusion = bf16[16,20,8192]{2,1,0:T(8,128)(2,1)S(1)} fusion(bf16[16,20,512]{2,1,0:T(8,128)(2,1)S(1)} %reshape.291, bf16[512,8192]{1,0:T(8,128)(2,1)} %param.8), kind=kOutput, calls=%fused_computation.10 | convolution fusion | flops 2686976000 | bytes 13959168 | tf_op jit(solution)/shard_map/srk,kn->srn/dot_general | solution.py:85
  203.7 78.9 %all_to_all.15 = bf16[16,20,8192]{2,1,0:T(8,128)(2,1)} all-to-all(bf16[16,20,8192]{2,1,0:T(8,128)(2,1)S(1)} %convolution_convert_fusion), channel_id=1, replica_groups=mesh['section'=2,'seq'=4,'tensor'=16] {'tensor'}, dimensions={0} | all-to-all | bytes 10485760 | tf_op jit(solution)/shard_map/all_to_all | solution.py:88
  282.5 4.8 %reduce_sum.71 = bf16[20,8192]{1,0:T(8,128)(2,1)} reduce(bf16[16,20,8192]{2,1,0:T(8,128)(2,1)} %all_to_all.15, bf16[]{:T(256)} %constant.50.clone.1), dimensions={0}, to_apply=%region_6.7 | reduce | flops 2457600 | bytes 5570562 | tf_op jit(solution)/shard_map/reduce_sum | solution.py:89
  (23 shorter events, 0.3 us)
Async XLA Ops:
  6.5 2.7 copy-start
  6.5 0.8 copy-start.2
  6.5 138.2 %all-gather.2.cloned.1.call-start = ((), (), s32[]{:S(2)}) async-start(), calls=%async_computation.3 | async-start | bytes 22282240 | tf_op jit(solution)/shard_map/all_gather | solution.py:70
  10.8 19.7 %all-to-all-start = ((bf16[8,2,64,512]{3,2,1,0:T(8,128)(2,1)}), bf16[8,2,64,512]{3,2,1,0:T(8,128)(2,1)S(1)}, u32[]{:S(2)}, u32[]{:S(2)}) async-start(bf16[8,2,64,512]{3,2,1,0:T(8,128)(2,1)} %bitcast.8), calls=%async_computation | async-start | bytes 2097152 | tf_op jit(solution)/shard_map/all_to_all | solution.py:61
  176.4 19.5 %all-to-all-start.1 = ((bf16[8,2,64,512]{3,2,1,0:T(8,128)(2,1)}), bf16[8,2,64,512]{3,2,1,0:T(8,128)(2,1)S(1)}, u32[]{:S(2)}, u32[]{:S(2)}) async-start(bf16[8,2,64,512]{3,2,1,0:T(8,128)(2,1)} %bitcast.16), calls=%async_computation.1 | async-start | bytes 2097152 | tf_op jit(solution)/shard_map/all_to_all | solution.py:82
  282.5 4.8 %copy-start.1 = (bf16[320,512]{1,0:T(8,128)(2,1)S(1)}, bf16[320,512]{1,0:T(8,128)(2,1)}, u32[]{:S(2)}) copy-start(bf16[320,512]{1,0:T(8,128)(2,1)} %param.5) | copy-start | bytes 983044
Sparse Core Ops, SparseCore 0:
  9.5 135.2 all-gather.1

commit v7 on v5

--- a/solution.py
+++ b/solution.py
@@ -79,8 +79,14 @@
         jnp.where(pick_a, jnp.arange(CAPC, dtype=jnp.int32)[None, None, :], 0), axis=-1
     )
     send_a = attended[send_a_idx]
-    recv_a = lax.all_to_all(send_a, ("section", "seq"), split_axis=0, concat_axis=0, tiled=True)
-    attended_rows = recv_a[own_owner, own_arrival].reshape(tensor_size, -1, cols)
+    by_shift = [send_a[group_index]]
+    for k in range(1, groups):
+        block = lax.dynamic_index_in_dim(send_a, (group_index + k) % groups, 0, keepdims=False)
+        pairs = [(s, (s + k) % groups) for s in range(groups)]
+        by_shift.append(lax.ppermute(block, ("section", "seq"), pairs))
+    recv_a = jnp.stack(by_shift)
+    shift_of = (group_index - own_owner) % groups
+    attended_rows = recv_a[shift_of, own_arrival].reshape(tensor_size, -1, cols)
 
     partial = jnp.einsum(
         "srk,kn->srn", attended_rows, out_weight, preferred_element_type=jnp.float32

time: 293 us -> 290 us (0.990)
  waiting for transfers between devices: 224 us -> 219 us
    all_to_all x1 -> x0, waiting for transfers between devices: 15.2 us -> none  [on_device(): lax.all_to_all(send_a, ('section', 'seq'), split_axis=0, concat_axis=0, t...]
    ppermute x0 -> x7, waiting for transfers between devices: none -> 8.95 us  [on_device(): by_shift.append(lax.ppermute(block, ('section', 'seq'), pairs))]
    ppermute x0 -> x7, starting transfers between devices: none -> 6.91 us  [on_device(): by_shift.append(lax.ppermute(block, ('section', 'seq'), pairs))]
    all_to_all x1 -> x0, starting transfers between devices: 4.25 us -> none  [on_device(): lax.all_to_all(send_a, ('section', 'seq'), split_axis=0, concat_axis=0, t...]
  transfers between devices with their start and end apart: 4 -> 10, of which waited for: 4 -> 7; matrix products, arithmetic and copies ran while one was open for 2% -> 2% of each run, Pallas kernels for 0% -> 0%
where the time goes in v7:
time: 290 us
  waiting for transfers between devices  219 us (76%)
  matrix products  38 us (13%)
  between operations  13.7 us (5%)
  starting transfers between devices  11.4 us (4%)
  local copies, waits for them, and re-layouts  6.12 us (2%)
    all_gather x1, waiting for transfers between devices, on_device(): rows = lax.all_gather(neighbours, 'tensor', axis=0, tiled=True)  113 us
    unnamed x3, waiting for transfers between devices  82.5 us
    dot_general x1, matrix products, on_device(): jnp.einsum('skd,cde->cske', rows, kv_weight, preferred_element_type=jnp.f...  26.7 us
    all_to_all x1, waiting for transfers between devices, on_device(): lax.all_to_all(send_q, ('section', 'seq'), split_axis=0, concat_axis=0, t...  14.9 us
    ppermute x7, waiting for transfers between devices, on_device(): by_shift.append(lax.ppermute(block, ('section', 'seq'), pairs))  8.95 us
    dot_general x1, matrix products, on_device(): jnp.einsum('srk,kn->srn', attended_rows, out_weight, preferred_element_ty...  8.72 us
    ppermute x7, starting transfers between devices, on_device(): by_shift.append(lax.ppermute(block, ('section', 'seq'), pairs))  6.91 us
  transfers between devices with their start and end apart: 10, of which 7 were waited for; matrix products, arithmetic and copies ran while one was open for 2% of the time, Pallas kernels for 0%

profile of v7, /device:TPU:0, one launch (start us, length us, event | category | flops | bytes accessed | tf_op | source)
XLA Modules:
  0.0 289.6 jit_solution(5920585559241900253)
XLA Ops:
  6.5 0.7 all-gather.2.cloned.1.call-update
  7.3 0.6 gather_fusion
  8.0 0.2 convert_reduce_fusion
  8.2 0.7 gather_fusion.1
  8.8 0.2 select_reduce_fusion
  9.0 0.6 gather_fusion.3
  9.8 0.1 fusion.13
  10.4 1.6 gather_fusion.2
  11.9 4.4 %all-to-all-start = ((bf16[8,2,64,512]{3,2,1,0:T(8,128)(2,1)}), bf16[8,2,64,512]{3,2,1,0:T(8,128)(2,1)S(1)}, u32[]{:S(2)}, u32[]{:S(2)}) async-start(bf16[8,2,64,512]{3,2,1,0:T(8,128)(2,1)} %bitcast.8), calls=%async_computation | async-start | bytes 2097152 | tf_op jit(solution)/shard_map/all_to_all | solution.py:61
  16.7 14.9 %all-to-all-done = bf16[8,2,64,512]{3,2,1,0:T(8,128)(2,1)S(1)} async-done(((bf16[8,2,64,512]{3,2,1,0:T(8,128)(2,1)}), bf16[8,2,64,512]{3,2,1,0:T(8,128)(2,1)S(1)}, u32[]{:S(2)}, u32[]{:S(2)}) %all-to-all-start) | async-done | bytes 1048608 | tf_op jit(solution)/shard_map/all_to_all | solution.py:61
  31.6 0.6 gather_fusion.4
  32.2 112.6 %all-gather.2.cloned.1.call-done = bf16[1280,8192]{1,0:T(8,128)(2,1)} async-done(((bf16[80,8192]{1,0:T(8,128)(2,1)}), bf16[1280,8192]{1,0:T(8,128)(2,1)}) %all-gather.2.cloned.1.call-update) | async-done | bytes 20971536 | tf_op jit(solution)/shard_map/all_gather | solution.py:70
  144.8 26.7 %convert_bitcast_fusion = bf16[2,5,256,512]{2,3,1,0:T(8,128)(2,1)S(1)} fusion(bf16[5,256,8192,1]{2,1,0,3:T(8,128)(2,1)} %bitcast.115, bf16[2,8192,512]{2,1,0:T(8,128)(2,1)} %param.7), kind=kOutput, calls=%fused_computation.12 | convolution fusion | flops 21476147200 | bytes 40370176 | tf_op jit(solution)/shard_map/skd,cde->cske/dot_general | solution.py:72
  171.5 0.2 fusion.30
  171.7 0.3 convolution_multiply_fusion
  172.0 0.4 fusion.31
  172.4 2.3 fusion.8
  174.8 0.6 gather_fusion.5
  175.4 0.1 dynamic-slice_bitcast_fusion
  175.5 1.6 collective-permute-start
  177.1 2.7 collective-permute-start.1
  179.9 0.4 collective-permute-start.2
  180.3 0.9 collective-permute-start.3
  181.2 0.4 collective-permute-start.4
  181.6 1.9 collective-permute-done
  183.5 1.0 collective-permute-done.1
  184.5 0.9 collective-permute-start.6
  185.4 0.4 collective-permute-done.2
  185.8 5.7 %collective-permute-done.4 = bf16[2,64,512]{2,1,0:T(8,128)(2,1)S(1)} collective-permute-done((bf16[2,64,512]{2,1,0:T(8,128)(2,1)S(1)}, bf16[2,64,512]{2,1,0:T(8,128)(2,1)S(1)}, u32[]{:S(2)}, u32[]{:S(2)}) %collective-permute-start.4) | collective-permute-done | bytes 131104 | tf_op jit(solution)/shard_map/ppermute | solution.py:86
  191.6 0.6 gather_fusion.6
  192.2 8.7 %convolution_convert_fusion = bf16[16,20,8192]{2,1,0:T(8,128)(2,1)} fusion(bf16[16,20,512]{2,1,0:T(8,128)(2,1)S(1)} %reshape.332, bf16[512,8192]{1,0:T(8,128)(2,1)} %param.8), kind=kOutput, calls=%fused_computation.10 | convolution fusion | flops 2686976000 | bytes 13959168 | tf_op jit(solution)/shard_map/srk,kn->srn/dot_general | solution.py:91
  201.0 81.8 %reduce-scatter.4.cloned.1.call-done = bf16[1,20,8192]{2,1,0:T(8,128)(2,1)} async-done(((bf16[16,20,8192]{2,1,0:T(8,128)(2,1)}), bf16[1,20,8192]{2,1,0:T(8,128)(2,1)}) %reduce-scatter.4.cloned.1.call-update) | async-done | bytes 327696
  (44 shorter events, 1.1 us)
Async XLA Ops:
  6.5 3.8 %copy-start = (bf16[320,512]{1,0:T(8,128)(2,1)S(1)}, bf16[320,512]{1,0:T(8,128)(2,1)}, u32[]{:S(2)}) copy-start(bf16[320,512]{1,0:T(8,128)(2,1)} %param.5) | copy-start | bytes 983044
  6.5 0.8 copy-start.2
  6.5 138.2 %all-gather.2.cloned.1.call-start = ((), (), s32[]{:S(2)}) async-start(), calls=%async_computation.2 | async-start | bytes 22282240 | tf_op jit(solution)/shard_map/all_gather | solution.py:70
  11.9 19.7 %all-to-all-start = ((bf16[8,2,64,512]{3,2,1,0:T(8,128)(2,1)}), bf16[8,2,64,512]{3,2,1,0:T(8,128)(2,1)S(1)}, u32[]{:S(2)}, u32[]{:S(2)}) async-start(bf16[8,2,64,512]{3,2,1,0:T(8,128)(2,1)} %bitcast.8), calls=%async_computation | async-start | bytes 2097152 | tf_op jit(solution)/shard_map/all_to_all | solution.py:61
  16.4 266.4 %reduce-scatter.4.cloned.1.call-start = ((), (), s32[]{:S(2)}) async-start(), calls=%async_computation.3 | async-start | bytes 6684672
  175.5 8.0 %collective-permute-start = (bf16[2,64,512]{2,1,0:T(8,128)(2,1)S(1)}, bf16[2,64,512]{2,1,0:T(8,128)(2,1)S(1)}, u32[]{:S(2)}, u32[]{:S(2)}) collective-permute-start(bf16[2,64,512]{2,1,0:T(8,128)(2,1)S(1)} %get-tuple-element.13), channel_id=1, source_target_pairs={{0,16},{16,32},{32,48},{48,64},{64,80},{80,96},{96,112},{112,0},{1... | collective-permute-start | bytes 393224 | tf_op jit(solution)/shard_map/ppermute | solution.py:86
  177.1 7.4 %collective-permute-start.1 = (bf16[2,64,512]{2,1,0:T(8,128)(2,1)S(1)}, bf16[2,64,512]{2,1,0:T(8,128)(2,1)S(1)}, u32[]{:S(2)}, u32[]{:S(2)}) collective-permute-start(bf16[2,64,512]{2,1,0:T(8,128)(2,1)S(1)} %get-tuple-element.12), channel_id=1, source_target_pairs={{0,32},{16,48},{32,64},{48,80},{64,96},{80,112},{96,0},{112,16},{1... | collective-permute-start | bytes 393224 | tf_op jit(solution)/shard_map/ppermute | solution.py:86
  179.9 5.9 %collective-permute-start.2 = (bf16[2,64,512]{2,1,0:T(8,128)(2,1)S(1)}, bf16[2,64,512]{2,1,0:T(8,128)(2,1)S(1)}, u32[]{:S(2)}, u32[]{:S(2)}) collective-permute-start(bf16[2,64,512]{2,1,0:T(8,128)(2,1)S(1)} %get-tuple-element.11), channel_id=1, source_target_pairs={{0,48},{16,64},{32,80},{48,96},{64,112},{80,0},{96,16},{112,32},{1... | collective-permute-start | bytes 393224 | tf_op jit(solution)/shard_map/ppermute | solution.py:86
  180.3 5.5 %collective-permute-start.3 = (bf16[2,64,512]{2,1,0:T(8,128)(2,1)S(1)}, bf16[2,64,512]{2,1,0:T(8,128)(2,1)S(1)}, u32[]{:S(2)}, u32[]{:S(2)}) collective-permute-start(bf16[2,64,512]{2,1,0:T(8,128)(2,1)S(1)} %get-tuple-element.10), channel_id=1, source_target_pairs={{0,64},{16,80},{32,96},{48,112},{64,0},{80,16},{96,32},{112,48},{1... | collective-permute-start | bytes 393224 | tf_op jit(solution)/shard_map/ppermute | solution.py:86
  181.2 10.3 %collective-permute-start.4 = (bf16[2,64,512]{2,1,0:T(8,128)(2,1)S(1)}, bf16[2,64,512]{2,1,0:T(8,128)(2,1)S(1)}, u32[]{:S(2)}, u32[]{:S(2)}) collective-permute-start(bf16[2,64,512]{2,1,0:T(8,128)(2,1)S(1)} %get-tuple-element.9), channel_id=1, source_target_pairs={{0,80},{16,96},{32,112},{48,0},{64,16},{80,32},{96,48},{112,64},{1... | collective-permute-start | bytes 393224 | tf_op jit(solution)/shard_map/ppermute | solution.py:86
  183.5 8.0 %collective-permute-start.5 = (bf16[2,64,512]{2,1,0:T(8,128)(2,1)S(1)}, bf16[2,64,512]{2,1,0:T(8,128)(2,1)S(1)}, u32[]{:S(2)}, u32[]{:S(2)}) collective-permute-start(bf16[2,64,512]{2,1,0:T(8,128)(2,1)S(1)} %get-tuple-element.8), channel_id=1, source_target_pairs={{0,96},{16,112},{32,0},{48,16},{64,32},{80,48},{96,64},{112,80},{1... | collective-permute-start | bytes 393224 | tf_op jit(solution)/shard_map/ppermute | solution.py:86
  184.5 7.0 %collective-permute-start.6 = (bf16[2,64,512]{2,1,0:T(8,128)(2,1)S(1)}, bf16[2,64,512]{2,1,0:T(8,128)(2,1)S(1)}, u32[]{:S(2)}, u32[]{:S(2)}) collective-permute-start(bf16[2,64,512]{2,1,0:T(8,128)(2,1)S(1)} %get-tuple-element.7), channel_id=1, source_target_pairs={{0,112},{16,0},{32,16},{48,32},{64,48},{80,64},{96,80},{112,96},{1... | collective-permute-start | bytes 393224 | tf_op jit(solution)/shard_map/ppermute | solution.py:86
  201.0 81.8 %copy-start.1 = (bf16[320,512]{1,0:T(8,128)(2,1)S(1)}, bf16[320,512]{1,0:T(8,128)(2,1)}, u32[]{:S(2)}) copy-start(bf16[320,512]{1,0:T(8,128)(2,1)} %param.5) | copy-start | bytes 983044
Sparse Core Ops, SparseCore 0:
  9.5 135.2 all-gather.1
  201.1 81.6 reduce-scatter.3

commit v8 on v7

--- a/solution.py
+++ b/solution.py
@@ -88,12 +88,17 @@
     shift_of = (group_index - own_owner) % groups
     attended_rows = recv_a[shift_of, own_arrival].reshape(tensor_size, -1, cols)
 
-    partial = jnp.einsum(
-        "srk,kn->srn", attended_rows, out_weight, preferred_element_type=jnp.float32
+    half = out_weight.shape[1] // 2
+    partial_a = jnp.einsum(
+        "srk,kn->srn", attended_rows, out_weight[:, :half], preferred_element_type=jnp.float32
     ).astype(jnp.bfloat16)
-    mixed = lax.psum_scatter(partial, "tensor", scatter_dimension=0, tiled=True)
-    return mixed.reshape(-1, out_weight.shape[1])
-
+    mixed_a = lax.psum_scatter(partial_a, "tensor", scatter_dimension=0, tiled=True)[0]
+    partial_b = jnp.einsum(
+        "srk,kn->srn", attended_rows, out_weight[:, half:], preferred_element_type=jnp.float32
+    ).astype(jnp.bfloat16)
+    pieces = lax.all_to_all(partial_b, "tensor", split_axis=0, concat_axis=0, tiled=True)
+    mixed_b = jnp.sum(pieces.astype(jnp.float32), axis=0).astype(jnp.bfloat16)
+    return jnp.concatenate([mixed_a, mixed_b], axis=1)
 
 def solution(mesh):
     placed = (

time: 290 us -> 304 us (1.048)
  blocking collectives: 0 us -> 50.9 us
  waiting for transfers between devices: 219 us -> 178 us
  other arithmetic: 1.38 us -> 4.44 us
    all_to_all x0 -> x1, blocking collectives: none -> 50.9 us  [on_device(): lax.all_to_all(partial_b, 'tensor', split_axis=0, concat_axis=0, tiled=True)]
    unnamed x3, waiting for transfers between devices: 82.5 us -> 41.3 us
    dot_general x1 -> x2, matrix products: 8.72 us -> 9.66 us  [the longest x1 5.66 us: on_device(): jnp.einsum('srk,kn->srn', attended_rows, out_weight[:, :half], preferred_...]
  transfers between devices with their start and end apart: 10 -> 10, of which waited for: 7 -> 7; matrix products, arithmetic and copies ran while one was open for 2% -> 4% of each run, Pallas kernels for 0% -> 0%
where the time goes in v8:
time: 304 us; the launch traced here: 303 us
  waiting for transfers between devices  178 us (59%)
  blocking collectives  50.9 us (17%)
  matrix products  39 us (13%)
  between operations  13.7 us (5%)
  starting transfers between devices  11.4 us (4%)
  local copies, waits for them, and re-layouts  6.12 us (2%)
  other arithmetic  4.44 us (1%)
    all_gather x1, waiting for transfers between devices, on_device(): rows = lax.all_gather(neighbours, 'tensor', axis=0, tiled=True)  113 us
    all_to_all x1, blocking collectives, on_device(): lax.all_to_all(partial_b, 'tensor', split_axis=0, concat_axis=0, tiled=True)  50.9 us
    unnamed x3, waiting for transfers between devices  41.3 us
    dot_general x1, matrix products, on_device(): jnp.einsum('skd,cde->cske', rows, kv_weight, preferred_element_type=jnp.f...  26.7 us
    all_to_all x1, waiting for transfers between devices, on_device(): lax.all_to_all(send_q, ('section', 'seq'), split_axis=0, concat_axis=0, t...  14.9 us
    ppermute x7, waiting for transfers between devices, on_device(): by_shift.append(lax.ppermute(block, ('section', 'seq'), pairs))  8.95 us
    ppermute x7, starting transfers between devices, on_device(): by_shift.append(lax.ppermute(block, ('section', 'seq'), pairs))  6.91 us
  transfers between devices with their start and end apart: 10, of which 7 were waited for; matrix products, arithmetic and copies ran while one was open for 4% of the time, Pallas kernels for 0%

profile of v8, /device:TPU:0, one launch (start us, length us, event | category | flops | bytes accessed | tf_op | source)
XLA Modules:
  0.0 303.3 jit_solution(10225576877030489376)
XLA Ops:
  6.5 0.7 all-gather.2.cloned.1.call-update
  7.3 0.6 gather_fusion
  8.0 0.2 convert_reduce_fusion
  8.2 0.7 gather_fusion.1
  9.0 0.6 gather_fusion.3
  10.4 1.6 gather_fusion.2
  11.9 4.4 %all-to-all-start = ((bf16[8,2,64,512]{3,2,1,0:T(8,128)(2,1)}), bf16[8,2,64,512]{3,2,1,0:T(8,128)(2,1)S(1)}, u32[]{:S(2)}, u32[]{:S(2)}) async-start(bf16[8,2,64,512]{3,2,1,0:T(8,128)(2,1)} %bitcast.8), calls=%async_computation | async-start | bytes 2097152 | tf_op jit(solution)/shard_map/all_to_all | solution.py:61
  16.7 14.9 %all-to-all-done = bf16[8,2,64,512]{3,2,1,0:T(8,128)(2,1)S(1)} async-done(((bf16[8,2,64,512]{3,2,1,0:T(8,128)(2,1)}), bf16[8,2,64,512]{3,2,1,0:T(8,128)(2,1)S(1)}, u32[]{:S(2)}, u32[]{:S(2)}) %all-to-all-start) | async-done | bytes 1048608 | tf_op jit(solution)/shard_map/all_to_all | solution.py:61
  31.6 0.6 gather_fusion.4
  32.2 112.6 %all-gather.2.cloned.1.call-done = bf16[1280,8192]{1,0:T(8,128)(2,1)} async-done(((bf16[80,8192]{1,0:T(8,128)(2,1)}), bf16[1280,8192]{1,0:T(8,128)(2,1)}) %all-gather.2.cloned.1.call-update) | async-done | bytes 20971536 | tf_op jit(solution)/shard_map/all_gather | solution.py:70
  144.8 26.7 %convert_bitcast_fusion = bf16[2,5,256,512]{2,3,1,0:T(8,128)(2,1)S(1)} fusion(bf16[5,256,8192,1]{2,1,0,3:T(8,128)(2,1)} %bitcast.120, bf16[2,8192,512]{2,1,0:T(8,128)(2,1)} %param.7), kind=kOutput, calls=%fused_computation.16 | convolution fusion | flops 21476147200 | bytes 40370176 | tf_op jit(solution)/shard_map/skd,cde->cske/dot_general | solution.py:72
  171.7 0.3 convolution_multiply_fusion
  172.0 0.4 fusion.34
  172.4 2.3 fusion.11
  174.8 0.6 gather_fusion.5
  175.5 1.6 collective-permute-start
  177.1 2.7 collective-permute-start.1
  179.9 0.4 collective-permute-start.2
  180.3 0.9 collective-permute-start.3
  181.2 0.4 collective-permute-start.4
  181.6 1.9 collective-permute-done
  183.5 1.0 collective-permute-done.1
  184.5 0.9 collective-permute-start.6
  185.4 0.4 collective-permute-done.2
  185.8 5.7 %collective-permute-done.4 = bf16[2,64,512]{2,1,0:T(8,128)(2,1)S(1)} collective-permute-done((bf16[2,64,512]{2,1,0:T(8,128)(2,1)S(1)}, bf16[2,64,512]{2,1,0:T(8,128)(2,1)S(1)}, u32[]{:S(2)}, u32[]{:S(2)}) %collective-permute-start.4) | collective-permute-done | bytes 131104 | tf_op jit(solution)/shard_map/ppermute | solution.py:86
  191.6 0.6 gather_fusion.6
  192.2 5.7 %convolution_convert_fusion.1 = bf16[16,20,4096]{2,1,0:T(8,128)(2,1)} fusion(bf16[16,20,512]{2,1,0:T(8,128)(2,1)S(1)} %reshape.329, bf16[512,8192]{1,0:T(8,128)(2,1)} %param.8), kind=kOutput, calls=%fused_computation.11 | convolution fusion | flops 1343488000 | bytes 7143424 | tf_op jit(solution)/shard_map/srk,kn->srn/dot_general | solution.py:92
  197.9 4.0 %convolution_convert_fusion = bf16[16,20,4096]{2,1,0:T(8,128)(2,1)S(1)} fusion(bf16[16,20,512]{2,1,0:T(8,128)(2,1)S(1)} %reshape.329, bf16[512,8192]{1,0:T(8,128)(2,1)} %param.8), kind=kOutput, calls=%fused_computation.10 | convolution fusion | flops 1343488000 | bytes 7143424 | tf_op jit(solution)/shard_map/srk,kn->srn/dot_general | solution.py:96
  201.9 50.9 %all_to_all.10 = bf16[16,20,4096]{2,1,0:T(8,128)(2,1)S(1)} all-to-all(bf16[16,20,4096]{2,1,0:T(8,128)(2,1)S(1)} %convolution_convert_fusion), channel_id=1, replica_groups=mesh['section'=2,'seq'=4,'tensor'=16] {'tensor'}, dimensions={0} | all-to-all | bytes 5242880 | tf_op jit(solution)/shard_map/all_to_all | solution.py:99
  252.8 1.3 reduce_sum.71
  254.1 40.5 %reduce-scatter.4.cloned.1.call-done = bf16[1,20,4096]{2,1,0:T(8,128)(2,1)} async-done(((bf16[16,20,4096]{2,1,0:T(8,128)(2,1)}), bf16[1,20,4096]{2,1,0:T(8,128)(2,1)}) %reduce-scatter.4.cloned.1.call-update) | async-done | bytes 163856
  294.6 1.8 pad_maximum_fusion
  (48 shorter events, 1.7 us)
Async XLA Ops:
  6.5 3.8 %copy-start = (bf16[320,512]{1,0:T(8,128)(2,1)S(1)}, bf16[320,512]{1,0:T(8,128)(2,1)}, u32[]{:S(2)}) copy-start(bf16[320,512]{1,0:T(8,128)(2,1)} %param.5) | copy-start | bytes 983044
  6.5 0.8 copy-start.2
  6.5 138.2 %all-gather.2.cloned.1.call-start = ((), (), s32[]{:S(2)}) async-start(), calls=%async_computation.3 | async-start | bytes 22282240 | tf_op jit(solution)/shard_map/all_gather | solution.py:70
  11.9 19.7 %all-to-all-start = ((bf16[8,2,64,512]{3,2,1,0:T(8,128)(2,1)}), bf16[8,2,64,512]{3,2,1,0:T(8,128)(2,1)S(1)}, u32[]{:S(2)}, u32[]{:S(2)}) async-start(bf16[8,2,64,512]{3,2,1,0:T(8,128)(2,1)} %bitcast.8), calls=%async_computation | async-start | bytes 2097152 | tf_op jit(solution)/shard_map/all_to_all | solution.py:61
  16.4 278.3 %reduce-scatter.4.cloned.1.call-start = ((), (), s32[]{:S(2)}) async-start(), calls=%async_computation.4 | async-start | bytes 3342336
  175.5 8.0 %collective-permute-start = (bf16[2,64,512]{2,1,0:T(8,128)(2,1)S(1)}, bf16[2,64,512]{2,1,0:T(8,128)(2,1)S(1)}, u32[]{:S(2)}, u32[]{:S(2)}) collective-permute-start(bf16[2,64,512]{2,1,0:T(8,128)(2,1)S(1)} %get-tuple-element.13), channel_id=1, source_target_pairs={{0,16},{16,32},{32,48},{48,64},{64,80},{80,96},{96,112},{112,0},{1... | collective-permute-start | bytes 393224 | tf_op jit(solution)/shard_map/ppermute | solution.py:86
  177.1 7.4 %collective-permute-start.1 = (bf16[2,64,512]{2,1,0:T(8,128)(2,1)S(1)}, bf16[2,64,512]{2,1,0:T(8,128)(2,1)S(1)}, u32[]{:S(2)}, u32[]{:S(2)}) collective-permute-start(bf16[2,64,512]{2,1,0:T(8,128)(2,1)S(1)} %get-tuple-element.12), channel_id=1, source_target_pairs={{0,32},{16,48},{32,64},{48,80},{64,96},{80,112},{96,0},{112,16},{1... | collective-permute-start | bytes 393224 | tf_op jit(solution)/shard_map/ppermute | solution.py:86
  179.9 5.9 %collective-permute-start.2 = (bf16[2,64,512]{2,1,0:T(8,128)(2,1)S(1)}, bf16[2,64,512]{2,1,0:T(8,128)(2,1)S(1)}, u32[]{:S(2)}, u32[]{:S(2)}) collective-permute-start(bf16[2,64,512]{2,1,0:T(8,128)(2,1)S(1)} %get-tuple-element.11), channel_id=1, source_target_pairs={{0,48},{16,64},{32,80},{48,96},{64,112},{80,0},{96,16},{112,32},{1... | collective-permute-start | bytes 393224 | tf_op jit(solution)/shard_map/ppermute | solution.py:86
  180.3 5.5 %collective-permute-start.3 = (bf16[2,64,512]{2,1,0:T(8,128)(2,1)S(1)}, bf16[2,64,512]{2,1,0:T(8,128)(2,1)S(1)}, u32[]{:S(2)}, u32[]{:S(2)}) collective-permute-start(bf16[2,64,512]{2,1,0:T(8,128)(2,1)S(1)} %get-tuple-element.10), channel_id=1, source_target_pairs={{0,64},{16,80},{32,96},{48,112},{64,0},{80,16},{96,32},{112,48},{1... | collective-permute-start | bytes 393224 | tf_op jit(solution)/shard_map/ppermute | solution.py:86
  181.2 10.3 %collective-permute-start.4 = (bf16[2,64,512]{2,1,0:T(8,128)(2,1)S(1)}, bf16[2,64,512]{2,1,0:T(8,128)(2,1)S(1)}, u32[]{:S(2)}, u32[]{:S(2)}) collective-permute-start(bf16[2,64,512]{2,1,0:T(8,128)(2,1)S(1)} %get-tuple-element.9), channel_id=1, source_target_pairs={{0,80},{16,96},{32,112},{48,0},{64,16},{80,32},{96,48},{112,64},{1... | collective-permute-start | bytes 393224 | tf_op jit(solution)/shard_map/ppermute | solution.py:86
  183.5 8.0 %collective-permute-start.5 = (bf16[2,64,512]{2,1,0:T(8,128)(2,1)S(1)}, bf16[2,64,512]{2,1,0:T(8,128)(2,1)S(1)}, u32[]{:S(2)}, u32[]{:S(2)}) collective-permute-start(bf16[2,64,512]{2,1,0:T(8,128)(2,1)S(1)} %get-tuple-element.8), channel_id=1, source_target_pairs={{0,96},{16,112},{32,0},{48,16},{64,32},{80,48},{96,64},{112,80},{1... | collective-permute-start | bytes 393224 | tf_op jit(solution)/shard_map/ppermute | solution.py:86
  184.5 7.0 %collective-permute-start.6 = (bf16[2,64,512]{2,1,0:T(8,128)(2,1)S(1)}, bf16[2,64,512]{2,1,0:T(8,128)(2,1)S(1)}, u32[]{:S(2)}, u32[]{:S(2)}) collective-permute-start(bf16[2,64,512]{2,1,0:T(8,128)(2,1)S(1)} %get-tuple-element.7), channel_id=1, source_target_pairs={{0,112},{16,0},{32,16},{48,32},{64,48},{80,64},{96,80},{112,96},{1... | collective-permute-start | bytes 393224 | tf_op jit(solution)/shard_map/ppermute | solution.py:86
  201.9 94.5 %copy-start.1 = (bf16[320,512]{1,0:T(8,128)(2,1)S(1)}, bf16[320,512]{1,0:T(8,128)(2,1)}, u32[]{:S(2)}) copy-start(bf16[320,512]{1,0:T(8,128)(2,1)} %param.5) | copy-start | bytes 983044
Sparse Core Ops, SparseCore 0:
  9.5 135.2 all-gather.1
  198.0 96.5 reduce-scatter.3

commit v9 on v7

--- a/solution.py
+++ b/solution.py
@@ -78,10 +78,9 @@
     send_a_idx = jnp.sum(
         jnp.where(pick_a, jnp.arange(CAPC, dtype=jnp.int32)[None, None, :], 0), axis=-1
     )
-    send_a = attended[send_a_idx]
-    by_shift = [send_a[group_index]]
+    by_shift = [attended[send_a_idx[group_index]]]
     for k in range(1, groups):
-        block = lax.dynamic_index_in_dim(send_a, (group_index + k) % groups, 0, keepdims=False)
+        block = attended[send_a_idx[(group_index + k) % groups]]
         pairs = [(s, (s + k) % groups) for s in range(groups)]
         by_shift.append(lax.ppermute(block, ("section", "seq"), pairs))
     recv_a = jnp.stack(by_shift)

time: 290 us -> 294 us (1.014)
  local copies, waits for them, and re-layouts: 6.12 us -> 9.99 us
    gather x1 -> x8, local copies, waits for them, and re-layouts: 0.61 us -> 4.43 us  [the longest x7 3.88 us: on_device(): block = attended[send_a_idx[(group_index + k) % groups]]]
  transfers between devices with their start and end apart: 10 -> 10, of which waited for: 7 -> 5; matrix products, arithmetic and copies ran while one was open for 2% -> 3% of each run, Pallas kernels for 0% -> 0%
where the time goes in v9:
time: 294 us
  waiting for transfers between devices  217 us (74%)
  matrix products  38.1 us (13%)
  between operations  13.9 us (5%)
  starting transfers between devices  13.5 us (5%)
  local copies, waits for them, and re-layouts  9.99 us (3%)
    all_gather x1, waiting for transfers between devices, on_device(): rows = lax.all_gather(neighbours, 'tensor', axis=0, tiled=True)  114 us
    unnamed x3, waiting for transfers between devices  82.2 us
    dot_general x1, matrix products, on_device(): jnp.einsum('skd,cde->cske', rows, kv_weight, preferred_element_type=jnp.f...  26.7 us
    all_to_all x1, waiting for transfers between devices, on_device(): lax.all_to_all(send_q, ('section', 'seq'), split_axis=0, concat_axis=0, t...  13.6 us
    ppermute x7, starting transfers between devices, on_device(): by_shift.append(lax.ppermute(block, ('section', 'seq'), pairs))  9.02 us
    dot_general x1, matrix products, on_device(): jnp.einsum('srk,kn->srn', attended_rows, out_weight, preferred_element_ty...  8.76 us
    ppermute x7, waiting for transfers between devices, on_device(): by_shift.append(lax.ppermute(block, ('section', 'seq'), pairs))  7.47 us
  transfers between devices with their start and end apart: 10, of which 5 were waited for; matrix products, arithmetic and copies ran while one was open for 3% of the time, Pallas kernels for 0%

profile of v9, /device:TPU:0, one launch (start us, length us, event | category | flops | bytes accessed | tf_op | source)
XLA Modules:
  0.0 293.7 jit_solution(14349235112250757149)
XLA Ops:
  6.5 0.7 all-gather.2.cloned.1.call-update
  7.5 0.6 gather_fusion
  8.3 0.7 gather_fusion.1
  9.4 1.6 gather_fusion.2
  11.0 4.4 %all-to-all-start = ((bf16[8,2,64,512]{3,2,1,0:T(8,128)(2,1)}), bf16[8,2,64,512]{3,2,1,0:T(8,128)(2,1)S(1)}, u32[]{:S(2)}, u32[]{:S(2)}) async-start(bf16[8,2,64,512]{3,2,1,0:T(8,128)(2,1)} %bitcast.8), calls=%async_computation | async-start | bytes 2097152 | tf_op jit(solution)/shard_map/all_to_all | solution.py:61
  15.6 0.6 gather_fusion.3
  17.1 13.6 %all-to-all-done = bf16[8,2,64,512]{3,2,1,0:T(8,128)(2,1)S(1)} async-done(((bf16[8,2,64,512]{3,2,1,0:T(8,128)(2,1)}), bf16[8,2,64,512]{3,2,1,0:T(8,128)(2,1)S(1)}, u32[]{:S(2)}, u32[]{:S(2)}) %all-to-all-start) | async-done | bytes 1048608 | tf_op jit(solution)/shard_map/all_to_all | solution.py:61
  30.7 0.6 gather_fusion.4
  31.3 113.5 %all-gather.2.cloned.1.call-done = bf16[1280,8192]{1,0:T(8,128)(2,1)} async-done(((bf16[80,8192]{1,0:T(8,128)(2,1)}), bf16[1280,8192]{1,0:T(8,128)(2,1)}) %all-gather.2.cloned.1.call-update) | async-done | bytes 20971536 | tf_op jit(solution)/shard_map/all_gather | solution.py:70
  144.8 26.7 %convert_bitcast_fusion = bf16[2,5,256,512]{2,3,1,0:T(8,128)(2,1)S(1)} fusion(bf16[5,256,8192,1]{2,1,0,3:T(8,128)(2,1)} %bitcast.136, bf16[2,8192,512]{2,1,0:T(8,128)(2,1)} %param.7), kind=kOutput, calls=%fused_computation.19 | convolution fusion | flops 21476147200 | bytes 40370176 | tf_op jit(solution)/shard_map/skd,cde->cske/dot_general | solution.py:72
  172.0 0.4 fusion.47
  172.4 2.3 fusion.8
  174.8 0.6 gather_fusion.5
  175.4 0.6 gather_fusion.6
  175.9 1.6 collective-permute-start
  177.5 0.6 gather_fusion.7
  178.1 2.7 collective-permute-start.1
  180.8 0.6 gather_fusion.8
  181.4 0.5 collective-permute-start.2
  181.9 0.6 gather_fusion.9
  182.4 0.9 collective-permute-start.3
  183.4 0.6 gather_fusion.10
  183.9 0.5 collective-permute-start.4
  184.5 0.6 gather_fusion.11
  185.0 0.6 gather_fusion.12
  185.6 1.3 collective-permute-start.5
  186.9 1.5 collective-permute-start.6
  188.5 5.0 %collective-permute-done.4 = bf16[2,64,512]{2,1,0:T(8,128)(2,1)S(1)} collective-permute-done((bf16[2,64,512]{2,1,0:T(8,128)(2,1)S(1)}, bf16[2,64,512]{2,1,0:T(8,128)(2,1)S(1)}, u32[]{:S(2)}, u32[]{:S(2)}) %collective-permute-start.4) | collective-permute-done | bytes 131104 | tf_op jit(solution)/shard_map/ppermute | solution.py:85
  193.5 2.5 collective-permute-done.6
  196.0 0.6 gather_fusion.13
  196.6 8.8 %convolution_convert_fusion = bf16[16,20,8192]{2,1,0:T(8,128)(2,1)} fusion(bf16[16,20,512]{2,1,0:T(8,128)(2,1)S(1)} %reshape.543, bf16[512,8192]{1,0:T(8,128)(2,1)} %param.8), kind=kOutput, calls=%fused_computation.17 | convolution fusion | flops 2686976000 | bytes 13959168 | tf_op jit(solution)/shard_map/srk,kn->srn/dot_general | solution.py:90
  205.4 81.4 %reduce-scatter.4.cloned.1.call-done = bf16[1,20,8192]{2,1,0:T(8,128)(2,1)} async-done(((bf16[16,20,8192]{2,1,0:T(8,128)(2,1)}), bf16[1,20,8192]{2,1,0:T(8,128)(2,1)}) %reduce-scatter.4.cloned.1.call-update) | async-done | bytes 327696
  (63 shorter events, 2.3 us)
Async XLA Ops:
  6.5 2.9 copy-start
  6.5 0.7 copy-start.2
  6.5 138.2 %all-gather.2.cloned.1.call-start = ((), (), s32[]{:S(2)}) async-start(), calls=%async_computation.2 | async-start | bytes 22282240 | tf_op jit(solution)/shard_map/all_gather | solution.py:70
  11.0 19.7 %all-to-all-start = ((bf16[8,2,64,512]{3,2,1,0:T(8,128)(2,1)}), bf16[8,2,64,512]{3,2,1,0:T(8,128)(2,1)S(1)}, u32[]{:S(2)}, u32[]{:S(2)}) async-start(bf16[8,2,64,512]{3,2,1,0:T(8,128)(2,1)} %bitcast.8), calls=%async_computation | async-start | bytes 2097152 | tf_op jit(solution)/shard_map/all_to_all | solution.py:61
  15.4 271.4 %reduce-scatter.4.cloned.1.call-start = ((), (), s32[]{:S(2)}) async-start(), calls=%async_computation.3 | async-start | bytes 6684672
  175.9 9.7 %collective-permute-start = (bf16[2,64,512]{2,1,0:T(8,128)(2,1)S(1)}, bf16[2,64,512]{2,1,0:T(8,128)(2,1)S(1)}, u32[]{:S(2)}, u32[]{:S(2)}) collective-permute-start(bf16[2,64,512]{2,1,0:T(8,128)(2,1)S(1)} %gather_fusion.6), channel_id=1, source_target_pairs={{0,16},{16,32},{32,48},{48,64},{64,80},{80,96},{96,112},{112,0},{1... | collective-permute-start | bytes 393224 | tf_op jit(solution)/shard_map/ppermute | solution.py:85
  178.1 8.9 %collective-permute-start.1 = (bf16[2,64,512]{2,1,0:T(8,128)(2,1)S(1)}, bf16[2,64,512]{2,1,0:T(8,128)(2,1)S(1)}, u32[]{:S(2)}, u32[]{:S(2)}) collective-permute-start(bf16[2,64,512]{2,1,0:T(8,128)(2,1)S(1)} %gather_fusion.7), channel_id=1, source_target_pairs={{0,32},{16,48},{32,64},{48,80},{64,96},{80,112},{96,0},{112,16},{1... | collective-permute-start | bytes 393224 | tf_op jit(solution)/shard_map/ppermute | solution.py:85
  181.4 7.0 %collective-permute-start.2 = (bf16[2,64,512]{2,1,0:T(8,128)(2,1)S(1)}, bf16[2,64,512]{2,1,0:T(8,128)(2,1)S(1)}, u32[]{:S(2)}, u32[]{:S(2)}) collective-permute-start(bf16[2,64,512]{2,1,0:T(8,128)(2,1)S(1)} %gather_fusion.8), channel_id=1, source_target_pairs={{0,48},{16,64},{32,80},{48,96},{64,112},{80,0},{96,16},{112,32},{1... | collective-permute-start | bytes 393224 | tf_op jit(solution)/shard_map/ppermute | solution.py:85
  182.4 6.0 %collective-permute-start.3 = (bf16[2,64,512]{2,1,0:T(8,128)(2,1)S(1)}, bf16[2,64,512]{2,1,0:T(8,128)(2,1)S(1)}, u32[]{:S(2)}, u32[]{:S(2)}) collective-permute-start(bf16[2,64,512]{2,1,0:T(8,128)(2,1)S(1)} %gather_fusion.9), channel_id=1, source_target_pairs={{0,64},{16,80},{32,96},{48,112},{64,0},{80,16},{96,32},{112,48},{1... | collective-permute-start | bytes 393224 | tf_op jit(solution)/shard_map/ppermute | solution.py:85
  183.9 9.5 %collective-permute-start.4 = (bf16[2,64,512]{2,1,0:T(8,128)(2,1)S(1)}, bf16[2,64,512]{2,1,0:T(8,128)(2,1)S(1)}, u32[]{:S(2)}, u32[]{:S(2)}) collective-permute-start(bf16[2,64,512]{2,1,0:T(8,128)(2,1)S(1)} %gather_fusion.10), channel_id=1, source_target_pairs={{0,80},{16,96},{32,112},{48,0},{64,16},{80,32},{96,48},{112,64},{1... | collective-permute-start | bytes 393224 | tf_op jit(solution)/shard_map/ppermute | solution.py:85
  185.6 7.8 %collective-permute-start.5 = (bf16[2,64,512]{2,1,0:T(8,128)(2,1)S(1)}, bf16[2,64,512]{2,1,0:T(8,128)(2,1)S(1)}, u32[]{:S(2)}, u32[]{:S(2)}) collective-permute-start(bf16[2,64,512]{2,1,0:T(8,128)(2,1)S(1)} %gather_fusion.11), channel_id=1, source_target_pairs={{0,96},{16,112},{32,0},{48,16},{64,32},{80,48},{96,64},{112,80},{1... | collective-permute-start | bytes 393224 | tf_op jit(solution)/shard_map/ppermute | solution.py:85
  186.9 9.0 %collective-permute-start.6 = (bf16[2,64,512]{2,1,0:T(8,128)(2,1)S(1)}, bf16[2,64,512]{2,1,0:T(8,128)(2,1)S(1)}, u32[]{:S(2)}, u32[]{:S(2)}) collective-permute-start(bf16[2,64,512]{2,1,0:T(8,128)(2,1)S(1)} %gather_fusion.12), channel_id=1, source_target_pairs={{0,112},{16,0},{32,16},{48,32},{64,48},{80,64},{96,80},{112,96},{1... | collective-permute-start | bytes 393224 | tf_op jit(solution)/shard_map/ppermute | solution.py:85
  205.4 81.5 %copy-start.1 = (bf16[320,512]{1,0:T(8,128)(2,1)S(1)}, bf16[320,512]{1,0:T(8,128)(2,1)}, u32[]{:S(2)}) copy-start(bf16[320,512]{1,0:T(8,128)(2,1)} %param.5) | copy-start | bytes 983044
Sparse Core Ops, SparseCore 0:
  9.5 135.2 all-gather.1
  205.5 81.2 reduce-scatter.3

commit v10 on v7

--- a/solution.py
+++ b/solution.py
@@ -22,7 +22,7 @@
     expo = jnp.exp(scores - peak)
     weights = (expo / jnp.sum(expo, axis=-1, keepdims=True)).astype(jnp.bfloat16)
     result = jnp.einsum(
-        "bhqk,bkhd->bqhd", weights, values, preferred_element_type=jnp.float32
+        "bhqk,bkhd->bhqd", weights, values, preferred_element_type=jnp.float32
     )
     return result.astype(jnp.bfloat16)
 
@@ -72,7 +72,7 @@
     kv = jnp.einsum("skd,cde->cske", rows, kv_weight, preferred_element_type=jnp.float32)
     kv = kv.astype(jnp.bfloat16).reshape(2, CAPC, KEYS, heads_local, HD)
     keys, values = kv[0], kv[1]
-    attended = attend(q_for_slot, keys, values).reshape(CAPC, SPAN, cols)
+    attended = attend(q_for_slot, keys, values)
 
     pick_a = (slot_group[None, None, :] == peer_ids) & (slot_place[None, None, :] == place_ids)
     send_a_idx = jnp.sum(
@@ -86,7 +86,8 @@
         by_shift.append(lax.ppermute(block, ("section", "seq"), pairs))
     recv_a = jnp.stack(by_shift)
     shift_of = (group_index - own_owner) % groups
-    attended_rows = recv_a[shift_of, own_arrival].reshape(tensor_size, -1, cols)
+    attended_rows = jnp.swapaxes(recv_a[shift_of, own_arrival], 1, 2)
+    attended_rows = attended_rows.reshape(tensor_size, -1, cols)
 
     partial = jnp.einsum(
         "srk,kn->srn", attended_rows, out_weight, preferred_element_type=jnp.float32

time: 290 us -> 290 us (level)
  no operation moved by 1% of the time
where the time goes in v10:
time: 290 us
  waiting for transfers between devices  219 us (76%)
  matrix products  38.1 us (13%)
  between operations  13.7 us (5%)
  starting transfers between devices  11.4 us (4%)
  local copies, waits for them, and re-layouts  6.65 us (2%)
    all_gather x1, waiting for transfers between devices, on_device(): rows = lax.all_gather(neighbours, 'tensor', axis=0, tiled=True)  113 us
    unnamed x3, waiting for transfers between devices  82.5 us
    dot_general x1, matrix products, on_device(): jnp.einsum('skd,cde->cske', rows, kv_weight, preferred_element_type=jnp.f...  26.7 us
    all_to_all x1, waiting for transfers between devices, on_device(): lax.all_to_all(send_q, ('section', 'seq'), split_axis=0, concat_axis=0, t...  14.9 us
    ppermute x7, waiting for transfers between devices, on_device(): by_shift.append(lax.ppermute(block, ('section', 'seq'), pairs))  8.91 us
    dot_general x1, matrix products, on_device(): jnp.einsum('srk,kn->srn', attended_rows, out_weight, preferred_element_ty...  8.76 us
    ppermute x7, starting transfers between devices, on_device(): by_shift.append(lax.ppermute(block, ('section', 'seq'), pairs))  6.91 us
  transfers between devices with their start and end apart: 10, of which 7 were waited for; matrix products, arithmetic and copies ran while one was open for 2% of the time, Pallas kernels for 0%

profile of v10, /device:TPU:0, one launch (start us, length us, event | category | flops | bytes accessed | tf_op | source)
XLA Modules:
  0.0 290.1 jit_solution(11920225293426894058)
XLA Ops:
  6.5 0.7 all-gather.2.cloned.1.call-update
  7.3 0.6 gather_fusion
  8.0 0.2 convert_reduce_fusion
  8.2 0.7 gather_fusion.1
  8.8 0.2 select_reduce_fusion
  9.0 0.6 gather_fusion.3
  10.4 1.6 gather_fusion.2
  11.9 4.4 %all-to-all-start = ((bf16[8,2,64,512]{3,2,1,0:T(8,128)(2,1)}), bf16[8,2,64,512]{3,2,1,0:T(8,128)(2,1)S(1)}, u32[]{:S(2)}, u32[]{:S(2)}) async-start(bf16[8,2,64,512]{3,2,1,0:T(8,128)(2,1)} %bitcast.3), calls=%async_computation | async-start | bytes 2097152 | tf_op jit(solution)/shard_map/all_to_all | solution.py:61
  16.7 14.9 %all-to-all-done = bf16[8,2,64,512]{3,2,1,0:T(8,128)(2,1)S(1)} async-done(((bf16[8,2,64,512]{3,2,1,0:T(8,128)(2,1)}), bf16[8,2,64,512]{3,2,1,0:T(8,128)(2,1)S(1)}, u32[]{:S(2)}, u32[]{:S(2)}) %all-to-all-start) | async-done | bytes 1048608 | tf_op jit(solution)/shard_map/all_to_all | solution.py:61
  31.6 0.6 gather_fusion.4
  32.2 112.6 %all-gather.2.cloned.1.call-done = bf16[1280,8192]{1,0:T(8,128)(2,1)} async-done(((bf16[80,8192]{1,0:T(8,128)(2,1)}), bf16[1280,8192]{1,0:T(8,128)(2,1)}) %all-gather.2.cloned.1.call-update) | async-done | bytes 20971536 | tf_op jit(solution)/shard_map/all_gather | solution.py:70
  144.8 26.7 %convert_bitcast_fusion = bf16[2,5,256,512]{2,3,1,0:T(8,128)(2,1)S(1)} fusion(bf16[5,256,8192,1]{2,1,0,3:T(8,128)(2,1)} %bitcast.110, bf16[2,8192,512]{2,1,0:T(8,128)(2,1)} %param.7), kind=kOutput, calls=%fused_computation.12 | convolution fusion | flops 21476147200 | bytes 40370176 | tf_op jit(solution)/shard_map/skd,cde->cske/dot_general | solution.py:72
  171.5 0.2 fusion.29
  171.7 0.3 convolution_multiply_fusion
  172.0 0.4 fusion.30
  172.4 2.3 convolution_convert_fusion.1
  174.7 0.8 gather_fusion.5
  175.6 1.6 collective-permute-start
  177.2 2.7 collective-permute-start.1
  179.9 0.4 collective-permute-start.2
  180.4 0.9 collective-permute-start.3
  181.2 0.4 collective-permute-start.4
  181.7 1.9 collective-permute-done
  183.6 1.0 collective-permute-done.1
  184.6 0.9 collective-permute-start.6
  185.4 0.4 collective-permute-done.2
  185.9 5.7 %collective-permute-done.4 = bf16[2,4,64,128]{3,2,1,0:T(8,128)(2,1)S(1)} collective-permute-done((bf16[2,4,64,128]{3,2,1,0:T(8,128)(2,1)S(1)}, bf16[2,4,64,128]{3,2,1,0:T(8,128)(2,1)S(1)}, u32[]{:S(2)}, u32[]{:S(2)}) %collective-permute-start.4) | collective-permute-done | bytes 131104 | tf_op jit(solution)/shard_map/ppermute | solution.py:86
  191.7 0.6 gather_fusion.6
  192.3 0.3 copy.38
  192.6 0.1 reshape.328
  192.7 8.8 %convolution_convert_fusion = bf16[16,20,8192]{2,1,0:T(8,128)(2,1)} fusion(bf16[16,20,512]{2,1,0:T(8,128)(2,1)S(1)} %reshape.328, bf16[512,8192]{1,0:T(8,128)(2,1)} %param.8), kind=kOutput, calls=%fused_computation.10 | convolution fusion | flops 2686976000 | bytes 13959168 | tf_op jit(solution)/shard_map/srk,kn->srn/dot_general | solution.py:92
  201.5 81.7 %reduce-scatter.4.cloned.1.call-done = bf16[1,20,8192]{2,1,0:T(8,128)(2,1)} async-done(((bf16[16,20,8192]{2,1,0:T(8,128)(2,1)}), bf16[1,20,8192]{2,1,0:T(8,128)(2,1)}) %reduce-scatter.4.cloned.1.call-update) | async-done | bytes 327696
  (44 shorter events, 1.2 us)
Async XLA Ops:
  6.5 3.8 %copy-start = (bf16[320,512]{1,0:T(8,128)(2,1)S(1)}, bf16[320,512]{1,0:T(8,128)(2,1)}, u32[]{:S(2)}) copy-start(bf16[320,512]{1,0:T(8,128)(2,1)} %param.5) | copy-start | bytes 983044
  6.5 0.8 copy-start.2
  6.5 138.2 %all-gather.2.cloned.1.call-start = ((), (), s32[]{:S(2)}) async-start(), calls=%async_computation.2 | async-start | bytes 22282240 | tf_op jit(solution)/shard_map/all_gather | solution.py:70
  11.9 19.7 %all-to-all-start = ((bf16[8,2,64,512]{3,2,1,0:T(8,128)(2,1)}), bf16[8,2,64,512]{3,2,1,0:T(8,128)(2,1)S(1)}, u32[]{:S(2)}, u32[]{:S(2)}) async-start(bf16[8,2,64,512]{3,2,1,0:T(8,128)(2,1)} %bitcast.3), calls=%async_computation | async-start | bytes 2097152 | tf_op jit(solution)/shard_map/all_to_all | solution.py:61
  16.4 266.9 %reduce-scatter.4.cloned.1.call-start = ((), (), s32[]{:S(2)}) async-start(), calls=%async_computation.3 | async-start | bytes 6684672
  175.6 8.0 %collective-permute-start = (bf16[2,4,64,128]{3,2,1,0:T(8,128)(2,1)S(1)}, bf16[2,4,64,128]{3,2,1,0:T(8,128)(2,1)S(1)}, u32[]{:S(2)}, u32[]{:S(2)}) collective-permute-start(bf16[2,4,64,128]{3,2,1,0:T(8,128)(2,1)S(1)} %get-tuple-element.13), channel_id=1, source_target_pairs={{0,16},{16,32},{32,48},{48,64},{64,80},{80,96},{96,112},{112,0},{1... | collective-permute-start | bytes 393224 | tf_op jit(solution)/shard_map/ppermute | solution.py:86
  177.2 7.4 %collective-permute-start.1 = (bf16[2,4,64,128]{3,2,1,0:T(8,128)(2,1)S(1)}, bf16[2,4,64,128]{3,2,1,0:T(8,128)(2,1)S(1)}, u32[]{:S(2)}, u32[]{:S(2)}) collective-permute-start(bf16[2,4,64,128]{3,2,1,0:T(8,128)(2,1)S(1)} %get-tuple-element.12), channel_id=1, source_target_pairs={{0,32},{16,48},{32,64},{48,80},{64,96},{80,112},{96,0},{112,16},{1... | collective-permute-start | bytes 393224 | tf_op jit(solution)/shard_map/ppermute | solution.py:86
  179.9 5.9 %collective-permute-start.2 = (bf16[2,4,64,128]{3,2,1,0:T(8,128)(2,1)S(1)}, bf16[2,4,64,128]{3,2,1,0:T(8,128)(2,1)S(1)}, u32[]{:S(2)}, u32[]{:S(2)}) collective-permute-start(bf16[2,4,64,128]{3,2,1,0:T(8,128)(2,1)S(1)} %get-tuple-element.11), channel_id=1, source_target_pairs={{0,48},{16,64},{32,80},{48,96},{64,112},{80,0},{96,16},{112,32},{1... | collective-permute-start | bytes 393224 | tf_op jit(solution)/shard_map/ppermute | solution.py:86
  180.4 5.5 %collective-permute-start.3 = (bf16[2,4,64,128]{3,2,1,0:T(8,128)(2,1)S(1)}, bf16[2,4,64,128]{3,2,1,0:T(8,128)(2,1)S(1)}, u32[]{:S(2)}, u32[]{:S(2)}) collective-permute-start(bf16[2,4,64,128]{3,2,1,0:T(8,128)(2,1)S(1)} %get-tuple-element.10), channel_id=1, source_target_pairs={{0,64},{16,80},{32,96},{48,112},{64,0},{80,16},{96,32},{112,48},{1... | collective-permute-start | bytes 393224 | tf_op jit(solution)/shard_map/ppermute | solution.py:86
  181.2 10.3 %collective-permute-start.4 = (bf16[2,4,64,128]{3,2,1,0:T(8,128)(2,1)S(1)}, bf16[2,4,64,128]{3,2,1,0:T(8,128)(2,1)S(1)}, u32[]{:S(2)}, u32[]{:S(2)}) collective-permute-start(bf16[2,4,64,128]{3,2,1,0:T(8,128)(2,1)S(1)} %get-tuple-element.9), channel_id=1, source_target_pairs={{0,80},{16,96},{32,112},{48,0},{64,16},{80,32},{96,48},{112,64},{1... | collective-permute-start | bytes 393224 | tf_op jit(solution)/shard_map/ppermute | solution.py:86
  183.6 8.0 %collective-permute-start.5 = (bf16[2,4,64,128]{3,2,1,0:T(8,128)(2,1)S(1)}, bf16[2,4,64,128]{3,2,1,0:T(8,128)(2,1)S(1)}, u32[]{:S(2)}, u32[]{:S(2)}) collective-permute-start(bf16[2,4,64,128]{3,2,1,0:T(8,128)(2,1)S(1)} %get-tuple-element.8), channel_id=1, source_target_pairs={{0,96},{16,112},{32,0},{48,16},{64,32},{80,48},{96,64},{112,80},{1... | collective-permute-start | bytes 393224 | tf_op jit(solution)/shard_map/ppermute | solution.py:86
  184.6 7.1 %collective-permute-start.6 = (bf16[2,4,64,128]{3,2,1,0:T(8,128)(2,1)S(1)}, bf16[2,4,64,128]{3,2,1,0:T(8,128)(2,1)S(1)}, u32[]{:S(2)}, u32[]{:S(2)}) collective-permute-start(bf16[2,4,64,128]{3,2,1,0:T(8,128)(2,1)S(1)} %get-tuple-element.7), channel_id=1, source_target_pairs={{0,112},{16,0},{32,16},{48,32},{64,48},{80,64},{96,80},{112,96},{1... | collective-permute-start | bytes 393224 | tf_op jit(solution)/shard_map/ppermute | solution.py:86
  201.5 81.7 %copy-start.1 = (bf16[320,512]{1,0:T(8,128)(2,1)S(1)}, bf16[320,512]{1,0:T(8,128)(2,1)}, u32[]{:S(2)}) copy-start(bf16[320,512]{1,0:T(8,128)(2,1)} %param.5) | copy-start | bytes 983044
Sparse Core Ops, SparseCore 0:
  9.5 135.2 all-gather.1
  201.6 81.5 reduce-scatter.3

commit v11 on v7

--- a/solution.py
+++ b/solution.py
@@ -58,14 +58,20 @@
     )
     query_blocks = queries.reshape(CH_DEV, SPAN, cols)
     send_q = query_blocks[send_q_idx]
-    recv_q = lax.all_to_all(send_q, ("section", "seq"), split_axis=0, concat_axis=0, tiled=True)
+    q_by_shift = [send_q[group_index]]
+    for k in range(1, groups):
+        block = lax.dynamic_index_in_dim(send_q, (group_index + k) % groups, 0, keepdims=False)
+        pairs = [(s, (s + k) % groups) for s in range(groups)]
+        q_by_shift.append(lax.ppermute(block, ("section", "seq"), pairs))
+    recv_q = jnp.stack(q_by_shift)
 
     my_slots = group_index * CAPC + jnp.arange(CAPC, dtype=jnp.int32)
     hit = slot_map[None, :] == my_slots[:, None]
     slot_span = jnp.sum(jnp.where(hit, span_ids[None, :], 0), axis=1)
     slot_group = slot_span // CH_DEV
     slot_place = arrival[slot_span]
-    q_for_slot = recv_q[slot_group, slot_place].reshape(CAPC, SPAN, heads_local, HD)
+    q_for_slot = recv_q[(group_index - slot_group) % groups, slot_place]
+    q_for_slot = q_for_slot.reshape(CAPC, SPAN, heads_local, HD)
 
     rows = lax.all_gather(neighbours, "tensor", axis=0, tiled=True)
     rows = rows.reshape(CAPC, KEYS, rows.shape[1])

time: 290 us -> 289 us (level)
    all_to_all x1 -> x0, waiting for transfers between devices: 14.9 us -> none  [on_device(): lax.all_to_all(send_q, ('section', 'seq'), split_axis=0, concat_axis=0, t...]
    ppermute x0 -> x7, waiting for transfers between devices: none -> 9.52 us  [on_device(): q_by_shift.append(lax.ppermute(block, ('section', 'seq'), pairs))]
    ppermute x0 -> x7, starting transfers between devices: none -> 6.53 us  [on_device(): q_by_shift.append(lax.ppermute(block, ('section', 'seq'), pairs))]
    all_to_all x1 -> x0, starting transfers between devices: 4.41 us -> none  [on_device(): lax.all_to_all(send_q, ('section', 'seq'), split_axis=0, concat_axis=0, t...]
    all_gather x1, waiting for transfers between devices: 113 us -> 117 us  [on_device(): rows = lax.all_gather(neighbours, 'tensor', axis=0, tiled=True)]
  transfers between devices with their start and end apart: 10 -> 16, of which waited for: 7 -> 12; matrix products, arithmetic and copies ran while one was open for 2% -> 2% of each run, Pallas kernels for 0% -> 0%
where the time goes in v11:
time: 289 us
  waiting for transfers between devices  217 us (75%)
  matrix products  38 us (13%)
  between operations  13.8 us (5%)
  starting transfers between devices  13.5 us (5%)
  local copies, waits for them, and re-layouts  5.33 us (2%)
    all_gather x1, waiting for transfers between devices, on_device(): rows = lax.all_gather(neighbours, 'tensor', axis=0, tiled=True)  117 us
    unnamed x3, waiting for transfers between devices  82 us
    dot_general x1, matrix products, on_device(): jnp.einsum('skd,cde->cske', rows, kv_weight, preferred_element_type=jnp.f...  26.7 us
    ppermute x7, waiting for transfers between devices, on_device(): q_by_shift.append(lax.ppermute(block, ('section', 'seq'), pairs))  9.52 us
    ppermute x7, waiting for transfers between devices, on_device(): by_shift.append(lax.ppermute(block, ('section', 'seq'), pairs))  8.93 us
    dot_general x1, matrix products, on_device(): jnp.einsum('srk,kn->srn', attended_rows, out_weight, preferred_element_ty...  8.7 us
    ppermute x7, starting transfers between devices, on_device(): by_shift.append(lax.ppermute(block, ('section', 'seq'), pairs))  6.93 us
    ppermute x7, starting transfers between devices, on_device(): q_by_shift.append(lax.ppermute(block, ('section', 'seq'), pairs))  6.53 us
  transfers between devices with their start and end apart: 16, of which 12 were waited for; matrix products, arithmetic and copies ran while one was open for 2% of the time, Pallas kernels for 0%

profile of v11, /device:TPU:0, one launch (start us, length us, event | category | flops | bytes accessed | tf_op | source)
XLA Modules:
  0.0 289.1 jit_solution(14220398571249133182)
XLA Ops:
  6.5 0.7 all-gather.2.cloned.1.call-update
  7.5 0.6 gather_fusion
  8.3 0.7 gather_fusion.1
  9.2 0.6 gather_fusion.3
  10.4 0.6 gather_fusion.2
  11.2 1.7 collective-permute-start
  12.9 2.7 collective-permute-start.1
  15.6 0.6 collective-permute-start.2
  16.2 0.7 collective-permute-start.3
  16.9 0.5 collective-permute-start.4
  17.5 0.9 collective-permute-done
  18.6 1.9 collective-permute-done.1
  20.7 0.7 collective-permute-done.2
  21.4 4.2 %collective-permute-done.4 = bf16[2,64,512]{2,1,0:T(8,128)(2,1)S(1)} collective-permute-done((bf16[2,64,512]{2,1,0:T(8,128)(2,1)S(1)}, bf16[2,64,512]{2,1,0:T(8,128)(2,1)S(1)}, u32[]{:S(2)}, u32[]{:S(2)}) %collective-permute-start.4) | collective-permute-done | bytes 131104 | tf_op jit(solution)/shard_map/ppermute | solution.py:65
  25.7 1.7 collective-permute-done.5
  27.5 0.6 gather_fusion.4
  28.1 116.7 %all-gather.2.cloned.1.call-done = bf16[1280,8192]{1,0:T(8,128)(2,1)} async-done(((bf16[80,8192]{1,0:T(8,128)(2,1)}), bf16[1280,8192]{1,0:T(8,128)(2,1)}) %all-gather.2.cloned.1.call-update) | async-done | bytes 20971536 | tf_op jit(solution)/shard_map/all_gather | solution.py:76
  144.8 26.7 %convert_bitcast_fusion = bf16[2,5,256,512]{2,3,1,0:T(8,128)(2,1)S(1)} fusion(bf16[5,256,8192,1]{2,1,0,3:T(8,128)(2,1)} %bitcast.146, bf16[2,8192,512]{2,1,0:T(8,128)(2,1)} %param.7), kind=kOutput, calls=%fused_computation.12 | convolution fusion | flops 21476147200 | bytes 40370176 | tf_op jit(solution)/shard_map/skd,cde->cske/dot_general | solution.py:78
  172.4 2.3 fusion.8
  174.8 0.6 gather_fusion.5
  175.6 1.5 collective-permute-start.7
  177.1 2.8 collective-permute-start.8
  179.9 0.5 collective-permute-start.9
  180.3 0.8 collective-permute-start.10
  181.2 0.5 collective-permute-start.11
  181.6 1.9 collective-permute-done.7
  183.6 0.9 collective-permute-done.8
  184.5 0.9 collective-permute-start.13
  185.8 5.7 %collective-permute-done.11 = bf16[2,64,512]{2,1,0:T(8,128)(2,1)S(1)} collective-permute-done((bf16[2,64,512]{2,1,0:T(8,128)(2,1)S(1)}, bf16[2,64,512]{2,1,0:T(8,128)(2,1)S(1)}, u32[]{:S(2)}, u32[]{:S(2)}) %collective-permute-start.11) | collective-permute-done | bytes 131104 | tf_op jit(solution)/shard_map/ppermute | solution.py:92
  191.6 0.6 gather_fusion.6
  192.2 8.7 %convolution_convert_fusion = bf16[16,20,8192]{2,1,0:T(8,128)(2,1)} fusion(bf16[16,20,512]{2,1,0:T(8,128)(2,1)S(1)} %reshape.368, bf16[512,8192]{1,0:T(8,128)(2,1)} %param.8), kind=kOutput, calls=%fused_computation.10 | convolution fusion | flops 2686976000 | bytes 13959168 | tf_op jit(solution)/shard_map/srk,kn->srn/dot_general | solution.py:97
  201.0 81.3 %reduce-scatter.4.cloned.1.call-done = bf16[1,20,8192]{2,1,0:T(8,128)(2,1)} async-done(((bf16[16,20,8192]{2,1,0:T(8,128)(2,1)}), bf16[1,20,8192]{2,1,0:T(8,128)(2,1)}) %reduce-scatter.4.cloned.1.call-update) | async-done | bytes 327696
  (64 shorter events, 3.7 us)
Async XLA Ops:
  6.5 3.9 %copy-start = (bf16[320,512]{1,0:T(8,128)(2,1)S(1)}, bf16[320,512]{1,0:T(8,128)(2,1)}, u32[]{:S(2)}) copy-start(bf16[320,512]{1,0:T(8,128)(2,1)} %param.5) | copy-start | bytes 983044
  6.5 0.9 copy-start.2
  6.5 138.2 %all-gather.2.cloned.1.call-start = ((), (), s32[]{:S(2)}) async-start(), calls=%async_computation.1 | async-start | bytes 22282240 | tf_op jit(solution)/shard_map/all_gather | solution.py:76
  7.3 275.0 %reduce-scatter.4.cloned.1.call-start = ((), (), s32[]{:S(2)}) async-start(), calls=%async_computation.2 | async-start | bytes 6684672
  11.2 7.2 %collective-permute-start = (bf16[2,64,512]{2,1,0:T(8,128)(2,1)S(1)}, bf16[2,64,512]{2,1,0:T(8,128)(2,1)S(1)}, u32[]{:S(2)}, u32[]{:S(2)}) collective-permute-start(bf16[2,64,512]{2,1,0:T(8,128)(2,1)S(1)} %get-tuple-element.21), channel_id=1, source_target_pairs={{0,16},{16,32},{32,48},{48,64},{64,80},{80,96},{96,112},{112,0},{1... | collective-permute-start | bytes 393224 | tf_op jit(solution)/shard_map/ppermute | solution.py:65
  12.9 7.6 %collective-permute-start.1 = (bf16[2,64,512]{2,1,0:T(8,128)(2,1)S(1)}, bf16[2,64,512]{2,1,0:T(8,128)(2,1)S(1)}, u32[]{:S(2)}, u32[]{:S(2)}) collective-permute-start(bf16[2,64,512]{2,1,0:T(8,128)(2,1)S(1)} %get-tuple-element.20), channel_id=1, source_target_pairs={{0,32},{16,48},{32,64},{48,80},{64,96},{80,112},{96,0},{112,16},{1... | collective-permute-start | bytes 393224 | tf_op jit(solution)/shard_map/ppermute | solution.py:65
  15.6 5.8 %collective-permute-start.2 = (bf16[2,64,512]{2,1,0:T(8,128)(2,1)S(1)}, bf16[2,64,512]{2,1,0:T(8,128)(2,1)S(1)}, u32[]{:S(2)}, u32[]{:S(2)}) collective-permute-start(bf16[2,64,512]{2,1,0:T(8,128)(2,1)S(1)} %get-tuple-element.19), channel_id=1, source_target_pairs={{0,48},{16,64},{32,80},{48,96},{64,112},{80,0},{96,16},{112,32},{1... | collective-permute-start | bytes 393224 | tf_op jit(solution)/shard_map/ppermute | solution.py:65
  16.2 5.2 %collective-permute-start.3 = (bf16[2,64,512]{2,1,0:T(8,128)(2,1)S(1)}, bf16[2,64,512]{2,1,0:T(8,128)(2,1)S(1)}, u32[]{:S(2)}, u32[]{:S(2)}) collective-permute-start(bf16[2,64,512]{2,1,0:T(8,128)(2,1)S(1)} %get-tuple-element.18), channel_id=1, source_target_pairs={{0,64},{16,80},{32,96},{48,112},{64,0},{80,16},{96,32},{112,48},{1... | collective-permute-start | bytes 393224 | tf_op jit(solution)/shard_map/ppermute | solution.py:65
  16.9 8.8 %collective-permute-start.4 = (bf16[2,64,512]{2,1,0:T(8,128)(2,1)S(1)}, bf16[2,64,512]{2,1,0:T(8,128)(2,1)S(1)}, u32[]{:S(2)}, u32[]{:S(2)}) collective-permute-start(bf16[2,64,512]{2,1,0:T(8,128)(2,1)S(1)} %get-tuple-element.17), channel_id=1, source_target_pairs={{0,80},{16,96},{32,112},{48,0},{64,16},{80,32},{96,48},{112,64},{1... | collective-permute-start | bytes 393224 | tf_op jit(solution)/shard_map/ppermute | solution.py:65
  18.4 8.9 %collective-permute-start.5 = (bf16[2,64,512]{2,1,0:T(8,128)(2,1)S(1)}, bf16[2,64,512]{2,1,0:T(8,128)(2,1)S(1)}, u32[]{:S(2)}, u32[]{:S(2)}) collective-permute-start(bf16[2,64,512]{2,1,0:T(8,128)(2,1)S(1)} %get-tuple-element.16), channel_id=1, source_target_pairs={{0,96},{16,112},{32,0},{48,16},{64,32},{80,48},{96,64},{112,80},{1... | collective-permute-start | bytes 393224 | tf_op jit(solution)/shard_map/ppermute | solution.py:65
  20.5 7.1 %collective-permute-start.6 = (bf16[2,64,512]{2,1,0:T(8,128)(2,1)S(1)}, bf16[2,64,512]{2,1,0:T(8,128)(2,1)S(1)}, u32[]{:S(2)}, u32[]{:S(2)}) collective-permute-start(bf16[2,64,512]{2,1,0:T(8,128)(2,1)S(1)} %get-tuple-element.15), channel_id=1, source_target_pairs={{0,112},{16,0},{32,16},{48,32},{64,48},{80,64},{96,80},{112,96},{1... | collective-permute-start | bytes 393224 | tf_op jit(solution)/shard_map/ppermute | solution.py:65
  175.6 8.0 %collective-permute-start.7 = (bf16[2,64,512]{2,1,0:T(8,128)(2,1)S(1)}, bf16[2,64,512]{2,1,0:T(8,128)(2,1)S(1)}, u32[]{:S(2)}, u32[]{:S(2)}) collective-permute-start(bf16[2,64,512]{2,1,0:T(8,128)(2,1)S(1)} %get-tuple-element.13), channel_id=1, source_target_pairs={{0,16},{16,32},{32,48},{48,64},{64,80},{80,96},{96,112},{112,0},{1... | collective-permute-start | bytes 393224 | tf_op jit(solution)/shard_map/ppermute | solution.py:92
  177.1 7.4 %collective-permute-start.8 = (bf16[2,64,512]{2,1,0:T(8,128)(2,1)S(1)}, bf16[2,64,512]{2,1,0:T(8,128)(2,1)S(1)}, u32[]{:S(2)}, u32[]{:S(2)}) collective-permute-start(bf16[2,64,512]{2,1,0:T(8,128)(2,1)S(1)} %get-tuple-element.12), channel_id=1, source_target_pairs={{0,32},{16,48},{32,64},{48,80},{64,96},{80,112},{96,0},{112,16},{1... | collective-permute-start | bytes 393224 | tf_op jit(solution)/shard_map/ppermute | solution.py:92
  179.9 5.9 %collective-permute-start.9 = (bf16[2,64,512]{2,1,0:T(8,128)(2,1)S(1)}, bf16[2,64,512]{2,1,0:T(8,128)(2,1)S(1)}, u32[]{:S(2)}, u32[]{:S(2)}) collective-permute-start(bf16[2,64,512]{2,1,0:T(8,128)(2,1)S(1)} %get-tuple-element.11), channel_id=1, source_target_pairs={{0,48},{16,64},{32,80},{48,96},{64,112},{80,0},{96,16},{112,32},{1... | collective-permute-start | bytes 393224 | tf_op jit(solution)/shard_map/ppermute | solution.py:92
  180.3 5.5 %collective-permute-start.10 = (bf16[2,64,512]{2,1,0:T(8,128)(2,1)S(1)}, bf16[2,64,512]{2,1,0:T(8,128)(2,1)S(1)}, u32[]{:S(2)}, u32[]{:S(2)}) collective-permute-start(bf16[2,64,512]{2,1,0:T(8,128)(2,1)S(1)} %get-tuple-element.10), channel_id=1, source_target_pairs={{0,64},{16,80},{32,96},{48,112},{64,0},{80,16},{96,32},{112,48},{1... | collective-permute-start | bytes 393224 | tf_op jit(solution)/shard_map/ppermute | solution.py:92
  181.2 10.3 %collective-permute-start.11 = (bf16[2,64,512]{2,1,0:T(8,128)(2,1)S(1)}, bf16[2,64,512]{2,1,0:T(8,128)(2,1)S(1)}, u32[]{:S(2)}, u32[]{:S(2)}) collective-permute-start(bf16[2,64,512]{2,1,0:T(8,128)(2,1)S(1)} %get-tuple-element.9), channel_id=1, source_target_pairs={{0,80},{16,96},{32,112},{48,0},{64,16},{80,32},{96,48},{112,64},{1... | collective-permute-start | bytes 393224 | tf_op jit(solution)/shard_map/ppermute | solution.py:92
  183.6 8.0 %collective-permute-start.12 = (bf16[2,64,512]{2,1,0:T(8,128)(2,1)S(1)}, bf16[2,64,512]{2,1,0:T(8,128)(2,1)S(1)}, u32[]{:S(2)}, u32[]{:S(2)}) collective-permute-start(bf16[2,64,512]{2,1,0:T(8,128)(2,1)S(1)} %get-tuple-element.8), channel_id=1, source_target_pairs={{0,96},{16,112},{32,0},{48,16},{64,32},{80,48},{96,64},{112,80},{1... | collective-permute-start | bytes 393224 | tf_op jit(solution)/shard_map/ppermute | solution.py:92
  184.5 7.1 %collective-permute-start.13 = (bf16[2,64,512]{2,1,0:T(8,128)(2,1)S(1)}, bf16[2,64,512]{2,1,0:T(8,128)(2,1)S(1)}, u32[]{:S(2)}, u32[]{:S(2)}) collective-permute-start(bf16[2,64,512]{2,1,0:T(8,128)(2,1)S(1)} %get-tuple-element.7), channel_id=1, source_target_pairs={{0,112},{16,0},{32,16},{48,32},{64,48},{80,64},{96,80},{112,96},{1... | collective-permute-start | bytes 393224 | tf_op jit(solution)/shard_map/ppermute | solution.py:92
  201.0 81.3 %copy-start.1 = (bf16[320,512]{1,0:T(8,128)(2,1)S(1)}, bf16[320,512]{1,0:T(8,128)(2,1)}, u32[]{:S(2)}) copy-start(bf16[320,512]{1,0:T(8,128)(2,1)} %param.5) | copy-start | bytes 983044
Sparse Core Ops, SparseCore 0:
  9.5 135.2 all-gather.1
  201.1 81.1 reduce-scatter.3
